TPU v7x, 256 devices: a whole 4x4x8 slice. The times are simulated.
256 devices in a mesh: group: 16 (over y_hi, x, core), leaf: 16 (over y_lo, z).
Axes of the slice: x: 4, y: 4 (y_hi: 2, y_lo: 2; y = y_hi * 2 + y_lo), z: 8, core: 2. Of those that a mesh axis runs over, the one named last changes fastest.
Arguments:
- leaf_mass: bfloat16 [256, 512, 512], P(('group', 'leaf')), may hold values from -23 to 23, as said below
- leaf_damp: bfloat16 [256, 512, 512], P(('group', 'leaf')), may hold values from -12 to 12, as said below
- mass_coupling: bfloat16 [256, 512, 1536], P(('group', 'leaf')), may hold values from -6 to 6
- damp_coupling: bfloat16 [256, 512, 1536], P(('group', 'leaf')), may hold values from -6 to 6
- leaf_modes: bfloat16 [256, 512, 1536], P(('group', 'leaf')), may hold values from -0.15625 to 0.15625
- interface_blocks: int32 [256, 12], P(('group', 'leaf')), may hold values from 0 to 11, each once within a row
- mid_modes: bfloat16 [16, 1536, 256], P('group', 'leaf'), may hold values from -0.15625 to 0.15625
- mid_constraint: bfloat16 [16, 1536, 1024], P('group', 'leaf'), may hold values from -0.109375 to 0.109375
Outputs:
- coupling_mass: float32 [256, 512, 256], P(('group', 'leaf'))
- coupling_damp: float32 [256, 512, 256], P(('group', 'leaf'))
- modal_mass: float32 [16, 256, 1280], P('group', 'leaf')
- modal_damp: float32 [16, 256, 1280], P('group', 'leaf')
- root_mass: float32 [1024, 1024], P(('group', 'leaf'))
- root_damp: float32 [1024, 1024], P(('group', 'leaf'))
Inputs may be any that keep to these rules, and one draw needn't show every extreme that they name: `interface_blocks`: each row is a permutation of 0 to 11. `leaf_mass`: each leaf's block is symmetric. `leaf_damp`: each leaf's block is symmetric.
All inputs are finite; a program needn't handle non-finite values.
Results may differ from a plain program's by a relative error of at most 0.0049.
Values may be sent and summed in bfloat16 or wider, within the bound.
No kernel may reach another device: no remote copies, remote signals or barrier semaphores. Data moves between devices by JAX's collectives and lax.ppermute only.
A program may use at most 128 MiB of HBM per device.

v0:
```python
import jax
import jax.numpy as jnp
from jax import lax
from jax.sharding import PartitionSpec as P


def to_middle(stacked, onehot, block_count, block_size):
    rows_total, width_total = stacked.shape
    moved = jnp.einsum(
        "lbk,bj->ljk",
        stacked.reshape(rows_total, block_count, block_size),
        onehot,
        preferred_element_type=jnp.float32,
    )
    return moved.astype(jnp.bfloat16).reshape(rows_total, width_total)


def left_product(first_operand, second_operand):
    return lax.dot_general(
        first_operand, second_operand, (((0,), (0,)), ((), ())), preferred_element_type=jnp.float32
    )


def body(
    leaf_mass,
    leaf_damp,
    mass_coupling,
    damp_coupling,
    leaf_modes,
    interface_blocks,
    mid_modes,
    mid_constraint,
):
    leaf_order = leaf_mass.shape[1]
    block_count = interface_blocks.shape[1]
    sep_width = leaf_modes.shape[2]
    block_size = sep_width // block_count
    mode_count = mid_modes.shape[2]
    root_width = mid_constraint.shape[2]
    basis_width = mode_count + root_width
    leaf_count = lax.axis_size("leaf")
    group_count = lax.axis_size("group")
    onehot = (
        interface_blocks[0][:, None] == jnp.arange(block_count, dtype=jnp.int32)[None, :]
    ).astype(jnp.bfloat16)
    placed = to_middle(
        jnp.concatenate([leaf_modes[0], mass_coupling[0], damp_coupling[0]], axis=0),
        onehot,
        block_count,
        block_size,
    )
    constraint = placed[:leaf_order]
    sides = placed[leaf_order:].astype(jnp.float32)
    product = jnp.dot(
        jnp.concatenate([leaf_mass[0], leaf_damp[0]], axis=0),
        constraint,
        preferred_element_type=jnp.float32,
    )
    half_work = (0.5 * product + sides).astype(jnp.bfloat16)
    full_work = (product + sides).astype(jnp.bfloat16)
    basis_rows = jnp.concatenate([mid_modes[0], mid_constraint[0]], axis=1)
    mode_basis = lax.all_gather(basis_rows, "leaf", axis=0, tiled=True)
    left_sum = jnp.dot(constraint, mode_basis, preferred_element_type=jnp.float32)
    right_sum = jnp.dot(half_work, mode_basis, preferred_element_type=jnp.float32)
    coupling = jnp.dot(full_work, mode_basis[:, :mode_count], preferred_element_type=jnp.float32)
    left_part = left_sum.astype(jnp.bfloat16)
    right_part = right_sum.astype(jnp.bfloat16)
    right_mass = right_part[:leaf_order]
    right_damp = right_part[leaf_order:]

    def projected_rows(first_row, amount, first_col):
        left_rows = lax.dynamic_slice_in_dim(left_part, first_row, amount, 1)
        right_rows = lax.dynamic_slice_in_dim(right_part, first_row, amount, 1)
        left_cols = left_part[:, first_col:]
        mass_term = left_product(left_rows, right_mass[:, first_col:]) + left_product(
            right_rows[:leaf_order], left_cols
        )
        damp_term = left_product(left_rows, right_damp[:, first_col:]) + left_product(
            right_rows[leaf_order:], left_cols
        )
        return jnp.concatenate([mass_term, damp_term], axis=1)

    modal_part = lax.psum_scatter(
        projected_rows(jnp.int32(0), mode_count // leaf_count * lax.axis_size("leaf"), 0),
        "leaf",
        scatter_dimension=0,
        tiled=True,
    )
    root_part = lax.psum_scatter(
        projected_rows(
            jnp.int32(0) + mode_count,
            root_width // (group_count * leaf_count) * lax.axis_size(("group", "leaf")),
            mode_count,
        ),
        ("group", "leaf"),
        scatter_dimension=0,
        tiled=True,
    )
    return (
        coupling[:leaf_order][None],
        coupling[leaf_order:][None],
        modal_part[:, :basis_width][None],
        modal_part[:, basis_width:][None],
        root_part[:, :root_width],
        root_part[:, root_width:],
    )


def solution(mesh):
    return jax.shard_map(
        body,
        mesh=mesh,
        in_specs=(
            P(("group", "leaf"), None, None),
            P(("group", "leaf"), None, None),
            P(("group", "leaf"), None, None),
            P(("group", "leaf"), None, None),
            P(("group", "leaf"), None, None),
            P(("group", "leaf"), None),
            P("group", "leaf", None),
            P("group", "leaf", None),
        ),
        out_specs=(
            P(("group", "leaf"), None, None),
            P(("group", "leaf"), None, None),
            P("group", "leaf", None),
            P("group", "leaf", None),
            P(("group", "leaf"), None),
            P(("group", "leaf"), None),
        ),
        check_vma=False,
    )
```

profile of v0, /device:TPU:2, one launch (start us, length us, event | category | flops | bytes accessed | tf_op | source)
XLA Modules:
  0.0 474.5 jit_solution(488696714255146082)
XLA Ops:
  7.2 0.0 all-gather.2.cloned.1.call-start
  7.2 1.6 pad_maximum_fusion.2
  8.9 0.0 all-gather.2.cloned.1.call-update
  8.9 0.0 all-reduce.3.cloned.1.call-start
  8.9 1.7 copy.41
  10.7 0.0 copy-start.5
  10.7 3.0 copy.44
  13.7 0.7 copy.42
  14.4 0.0 copy-start.6
  14.4 3.0 copy.45
  17.5 0.7 copy.40
  18.2 0.0 copy-start.9
  18.2 3.0 copy.43
  21.2 4.6 fusion
  25.8 1.2 copy.58
  27.1 2.2 copy-done.3
  29.3 0.1 slice.74
  29.4 0.7 copy.47
  30.1 5.2 %slice_convert_fusion = f32[1024,12,128]{2,0,1:T(8,128)} fusion(bf16[1536,12,128]{2,0,1:T(8,128)(2,1)} %bitcast.34), kind=kLoop, calls=%fused_computation.13 | loop fusion | flops 1572864 | bytes 9437184 | tf_op jit(solution)/shard_map/convert_element_type | solution.py:53
  35.3 6.6 %copy.48 = f32[1024,12,128]{0,2,1:T(8,128)} copy(f32[1024,12,128]{2,0,1:T(8,128)} %slice_convert_fusion) | data formatting | bytes 12582912 | tf_op jit(solution)/shard_map/convert_element_type | solution.py:53
  41.9 6.7 %copy.49 = f32[1024,1536]{1,0:T(8,128)} copy(f32[1024,1536]{0,1:T(8,128)} %bitcast.32) | data formatting | bytes 12582912 | tf_op jit(solution)/shard_map/convert_element_type | solution.py:53
  48.6 4.5 fusion.13
  53.0 35.5 %all-gather.2.cloned.1.call-done = bf16[1536,1280]{1,0:T(8,128)(2,1)} async-done(((bf16[96,1280]{1,0:T(8,128)(2,1)}), bf16[1536,1280]{1,0:T(8,128)(2,1)}) %all-gather.2.cloned.1.call-update) | async-done | bytes 3932176 | tf_op jit(solution)/shard_map/all_gather | solution.py:62
  88.6 4.5 convolution_convert_fusion.1
  93.1 1.3 copy-done.4
  94.4 6.6 %convolution_convert_fusion = bf16[1024,1280]{1,0:T(8,128)(2,1)S(1)} fusion(bf16[1536,1280]{1,0:T(8,128)(2,1)} %all-gather.2.cloned.1.call-done, f32[1024,1536]{1,0:T(8,128)S(1)} %copy-done.2, f32[1024,1536]{1,0:T(8,128)S(1)} %copy-done.4), kind=kOutput, calls=%fused_computation.11 | convolution fusion | flops 4032561152 | bytes 19136512 | tf_op jit(solution)/shard_map/dot_general | solution.py:64
  101.0 1.3 fusion.18
  102.3 1.3 fusion.21
  103.7 1.4 convolution_add_fusion.2
  105.1 1.4 convolution_add_fusion.3
  106.5 4.1 pad_maximum_fusion
  110.6 0.0 all-reduce.3.cloned.1.call-update
  110.6 0.0 reduce-scatter.3.cloned.1.call-start
  110.7 2.0 fusion.9
  112.6 0.1 copy-done.1
  112.8 0.5 fusion.11
  113.3 0.5 convolution_add_fusion
  113.8 0.5 convolution_add_fusion.1
  114.4 1.8 pad_maximum_fusion.1
  116.1 0.0 reduce-scatter.3.cloned.1.call-update
  116.2 6.3 %fusion.7 = f32[1024,256]{1,0:T(8,128)S(1)} fusion(f32[1024,1536]{1,0:T(8,128)} %fusion.13, f32[1024,1536]{1,0:T(8,128)} %copy.49, bf16[1536,1280]{1,0:T(8,128)(2,1)} %all-gather.2.cloned.1.call-done), kind=kOutput, calls=%fused_computation.12 | convolution fusion | flops 808452096 | bytes 14417920 | tf_op jit(solution)/shard_map/dot_general | solution.py:65
  122.5 1.0 slice_bitcast_fusion
  123.5 265.2 %all-reduce.3.cloned.1.call-done = f32[1024,2048]{0,1:T(8,128)} async-done(((f32[1024,2048]{0,1:T(8,128)}), f32[1024,2048]{0,1:T(8,128)}) %all-reduce.3.cloned.1.call-update) | async-done | bytes 8388624
  388.7 1.5 fusion.38
  390.2 0.8 copy.52
  391.0 0.8 copy.51
  391.8 74.5 %reduce-scatter.3.cloned.1.call-done = f32[16,2560]{1,0:T(8,128)} async-done(((f32[256,2560]{1,0:T(8,128)}), f32[16,2560]{1,0:T(8,128)}) %reduce-scatter.3.cloned.1.call-update) | async-done | bytes 163856 | tf_op jit(solution)/shard_map/reduce_scatter | solution.py:83
  466.3 1.6 slice_bitcast_fusion.2
  (14 shorter events, 0.0 us)
Async XLA Ops:
  7.2 81.4 %all-gather.2.cloned.1.call-start = ((), (), s32[]{:S(2)}) async-start(), calls=%async_computation.1 | async-start | bytes 4177920 | tf_op jit(solution)/shard_map/all_gather | solution.py:62
  8.9 379.8 %all-reduce.3.cloned.1.call-start = ((), (), s32[]{:S(2)}) async-start(), calls=%async_computation.3 | async-start | bytes 16777216
  10.7 3.0 copy-start.5
  14.4 3.0 copy-start.6
  18.2 3.0 copy-start.9
  27.1 2.2 copy-start.3
  41.9 6.7 %copy-start.7 = (bf16[1,512,512]{2,1,0:T(8,128)(2,1)S(1)}, bf16[1,512,512]{2,1,0:T(8,128)(2,1)}, u32[]{:S(2)}) copy-start(bf16[1,512,512]{2,1,0:T(8,128)(2,1)} %param.9) | copy-start | bytes 1572868
  41.9 6.7 %copy-start.8 = (bf16[1,512,512]{2,1,0:T(8,128)(2,1)S(1)}, bf16[1,512,512]{2,1,0:T(8,128)(2,1)}, u32[]{:S(2)}) copy-start(bf16[1,512,512]{2,1,0:T(8,128)(2,1)} %param.8) | copy-start | bytes 1572868
  88.6 4.5 copy-start.2
  88.6 5.8 %copy-start.4 = (f32[1024,1536]{1,0:T(8,128)S(1)}, f32[1024,1536]{1,0:T(8,128)}, u32[]{:S(2)}) copy-start(f32[1024,1536]{1,0:T(8,128)} %fusion.13) | copy-start | bytes 18874372
  101.0 4.1 copy-start
  110.6 355.8 %reduce-scatter.3.cloned.1.call-start = ((), (), s32[]{:S(2)}) async-start(), calls=%async_computation.2 | async-start | bytes 2785280 | tf_op jit(solution)/shard_map/reduce_scatter | solution.py:83
  110.6 2.1 copy-start.1
Sparse Core Ops, SparseCore 0:
  10.3 78.1 all-gather.1
  110.7 277.9 all-reduce.2
  391.3 75.0 reduce-scatter.2
where the time goes:
time: 475 us; the launch traced here: 474 us
  waiting for transfers between devices  375 us (79%)
  local copies, waits for them, and re-layouts  36.9 us (8%)
  matrix products  35.6 us (7%)
  between operations  13.9 us (3%)
  other arithmetic  12.6 us (3%)
    unnamed x4, waiting for transfers between devices  265 us
    reduce_scatter x1, waiting for transfers between devices, body(): lax.psum_scatter(projected_rows(jnp.int32(0), mode_count // leaf_count *...  74.5 us
    all_gather x1, waiting for transfers between devices, body(): mode_basis = lax.all_gather(basis_rows, 'leaf', axis=0, tiled=True)  35.5 us
    convert_element_type x2, local copies, waits for them, and re-layouts, body(): sides = placed[leaf_order:].astype(jnp.float32)  13.3 us
  transfers between devices with their start and end apart: 3, of which 3 were waited for; matrix products, arithmetic and copies ran while one was open for 12% of the time, Pallas kernels for 0%

commit v1 on v0

--- a/solution.py
+++ b/solution.py
@@ -86,15 +86,15 @@
         scatter_dimension=0,
         tiled=True,
     )
-    root_part = lax.psum_scatter(
-        projected_rows(
-            jnp.int32(0) + mode_count,
-            root_width // (group_count * leaf_count) * lax.axis_size(("group", "leaf")),
-            mode_count,
-        ),
-        ("group", "leaf"),
-        scatter_dimension=0,
-        tiled=True,
+    root_rows = projected_rows(jnp.int32(0) + mode_count, root_width, mode_count)
+    device_count = group_count * leaf_count
+    root_chunks = root_rows.reshape(device_count, root_width // device_count, 2 * root_width)
+    root_recv = lax.all_to_all(
+        root_chunks.astype(jnp.bfloat16), ("group", "leaf"), 0, 0, tiled=True
+    )
+    root_part = jnp.sum(
+        root_recv.reshape(device_count, root_width // device_count, 2 * root_width).astype(jnp.float32),
+        axis=0,
     )
     return (
         coupling[:leaf_order][None],

time: 475 us -> 271 us (0.57)
  waiting for transfers between devices: 375 us -> 144 us
  local copies, waits for them, and re-layouts: 36.9 us -> 48.1 us
  starting transfers between devices: 0.12 us -> 11 us
    unnamed x4 -> x2, waiting for transfers between devices: 265 us -> 0.03 us
    reduce_scatter x1, waiting for transfers between devices: 74.5 us -> 106 us  [body(): lax.psum_scatter(projected_rows(jnp.int32(0), mode_count // leaf_count *...]
    all_to_all x0 -> x1, starting transfers between devices: none -> 10.7 us  [body(): lax.all_to_all(root_chunks.astype(jnp.bfloat16), ('group', 'leaf'), 0, 0,...]
    convert_element_type x0 -> x1, local copies, waits for them, and re-layouts: none -> 7.2 us  [body(): root_chunks.astype(jnp.bfloat16)]
    concatenate x0 -> x1, local copies, waits for them, and re-layouts: none -> 6.52 us  [projected_rows(): return jnp.concatenate([mass_term, damp_term], axis=1)]
  transfers between devices with their start and end apart: 3 -> 3, of which waited for: 3 -> 3; matrix products, arithmetic and copies ran while one was open for 12% -> 21% of each run, Pallas kernels for 0% -> 0%
where the time goes in v1:
time: 271 us; the launch traced here: 268 us
  waiting for transfers between devices  144 us (53%)
  local copies, waits for them, and re-layouts  48.1 us (18%)
  matrix products  35.1 us (13%)
  other arithmetic  14.9 us (5%)
  between operations  14.2 us (5%)
  starting transfers between devices  11 us (4%)
    reduce_scatter x1, waiting for transfers between devices, body(): lax.psum_scatter(projected_rows(jnp.int32(0), mode_count // leaf_count *...  106 us
    all_gather x1, waiting for transfers between devices, body(): mode_basis = lax.all_gather(basis_rows, 'leaf', axis=0, tiled=True)  35.7 us
    convert_element_type x2, local copies, waits for them, and re-layouts, body(): sides = placed[leaf_order:].astype(jnp.float32)  13.3 us
    all_to_all x1, starting transfers between devices, body(): lax.all_to_all(root_chunks.astype(jnp.bfloat16), ('group', 'leaf'), 0, 0,...  10.7 us
    dot_general x8, matrix products, left_product(): lax.dot_general(first_operand, second_operand, (((0,), (0,)), ((), ())),...  9.09 us
    concatenate x3, local copies, waits for them, and re-layouts, body(): jnp.concatenate([leaf_modes[0], mass_coupling[0], damp_coupling[0]], axis=0)  9.04 us
    convert_element_type x1, local copies, waits for them, and re-layouts, body(): root_chunks.astype(jnp.bfloat16)  7.2 us
    unnamed x23, local copies, waits for them, and re-layouts  6.74 us
  transfers between devices with their start and end apart: 3, of which 3 were waited for; matrix products, arithmetic and copies ran while one was open for 21% of the time, Pallas kernels for 0%

profile of v1, /device:TPU:2, one launch (start us, length us, event | category | flops | bytes accessed | tf_op | source)
XLA Modules:
  0.0 267.5 jit_solution(10520976910876747802)
XLA Ops:
  7.2 0.0 all-gather.2.cloned.1.call-start
  7.2 1.6 pad_maximum_fusion.2
  8.9 0.0 all-gather.2.cloned.1.call-update
  8.9 1.7 copy.26
  10.6 0.0 copy-start.5
  10.6 3.0 %copy.29 = bf16[512,12,128]{2,1,0:T(8,128)(2,1)} copy(bf16[512,12,128]{0,2,1:T(8,128)(2,1)S(1)} %bitcast.33) | data formatting | bytes 3145728 | tf_op jit(solution)/shard_map/concatenate | solution.py:47
  13.6 0.7 copy.27
  14.3 0.0 copy-start.6
  14.3 3.0 %copy.30 = bf16[512,12,128]{2,1,0:T(8,128)(2,1)} copy(bf16[512,12,128]{0,2,1:T(8,128)(2,1)S(1)} %bitcast.34) | data formatting | bytes 3145728 | tf_op jit(solution)/shard_map/concatenate | solution.py:47
  17.4 0.7 copy.25
  18.1 0.0 copy-start.9
  18.1 3.0 %copy.28 = bf16[512,12,128]{2,1,0:T(8,128)(2,1)} copy(bf16[512,12,128]{0,2,1:T(8,128)(2,1)S(1)} %bitcast.35) | data formatting | bytes 3145728 | tf_op jit(solution)/shard_map/concatenate | solution.py:47
  21.1 4.6 %fusion = bf16[12,1536,128]{2,0,1:T(8,128)(2,1)S(1)} fusion(bf16[512,12,128]{2,1,0:T(8,128)(2,1)} %copy.30, bf16[512,12,128]{2,1,0:T(8,128)(2,1)} %copy.29, bf16[512,12,128]{2,1,0:T(8,128)(2,1)} %copy.28, s32[12]{0:T(128)S(1)} %bitcast.42), kind=kOutput, calls=%fused_computation.2 | convolution fusion | flops 70779024 | bytes 9437232 | tf_op jit(solution)/shard_map/lbk,bj->ljk/dot_general | solution.py:9
  25.7 1.2 copy.40
  27.0 2.2 copy-done.3
  29.2 0.1 slice.74
  29.3 0.7 copy.32
  30.0 5.1 %slice_convert_fusion = f32[1024,12,128]{2,0,1:T(8,128)} fusion(bf16[1536,12,128]{2,0,1:T(8,128)(2,1)} %bitcast.32), kind=kLoop, calls=%fused_computation.16 | loop fusion | flops 1572864 | bytes 9437184 | tf_op jit(solution)/shard_map/convert_element_type | solution.py:53
  35.1 6.6 %copy.33 = f32[1024,12,128]{0,2,1:T(8,128)} copy(f32[1024,12,128]{2,0,1:T(8,128)} %slice_convert_fusion) | data formatting | bytes 12582912 | tf_op jit(solution)/shard_map/convert_element_type | solution.py:53
  41.7 6.7 %copy.34 = f32[1024,1536]{1,0:T(8,128)} copy(f32[1024,1536]{0,1:T(8,128)} %bitcast.30) | data formatting | bytes 12582912 | tf_op jit(solution)/shard_map/convert_element_type | solution.py:53
  48.4 4.5 %fusion.13 = f32[1024,1536]{1,0:T(8,128)} fusion(bf16[512,1536]{0,1:T(8,128)(2,1)S(1)} %bitcast.36, bf16[512,512]{1,0:T(8,128)(2,1)S(1)} %bitcast.40, bf16[512,512]{1,0:T(8,128)(2,1)S(1)} %bitcast.41), kind=kOutput, calls=%fused_computation.26 | convolution fusion | flops 1612709888 | bytes 8912896 | tf_op jit(solution)/shard_map/dot_general | solution.py:54
  52.9 35.7 %all-gather.2.cloned.1.call-done = bf16[1536,1280]{1,0:T(8,128)(2,1)} async-done(((bf16[96,1280]{1,0:T(8,128)(2,1)}), bf16[1536,1280]{1,0:T(8,128)(2,1)}) %all-gather.2.cloned.1.call-update) | async-done | bytes 3932176 | tf_op jit(solution)/shard_map/all_gather | solution.py:62
  88.6 4.5 %convolution_convert_fusion.1 = bf16[512,1280]{1,0:T(8,128)(2,1)S(1)} fusion(bf16[512,1536]{0,1:T(8,128)(2,1)S(1)} %bitcast.37, bf16[1536,1280]{1,0:T(8,128)(2,1)} %all-gather.2.cloned.1.call-done), kind=kOutput, calls=%fused_computation.18 | convolution fusion | flops 2013921280 | bytes 6815744 | tf_op jit(solution)/shard_map/dot_general | solution.py:63
  93.1 1.3 copy-done.4
  94.4 6.6 %convolution_convert_fusion = bf16[1024,1280]{1,0:T(8,128)(2,1)S(1)} fusion(bf16[1536,1280]{1,0:T(8,128)(2,1)} %all-gather.2.cloned.1.call-done, f32[1024,1536]{1,0:T(8,128)S(1)} %copy-done, f32[1024,1536]{1,0:T(8,128)S(1)} %copy-done.4), kind=kOutput, calls=%fused_computation.14 | convolution fusion | flops 4032561152 | bytes 19136512 | tf_op jit(solution)/shard_map/dot_general | solution.py:64
  101.0 1.3 fusion.18
  102.3 1.3 fusion.21
  103.7 1.4 add_convert_fusion.2
  105.1 1.4 add_convert_fusion.3
  106.5 2.4 pad_maximum_fusion
  108.9 6.5 %copy.36 = bf16[1024,2048]{1,0:T(8,128)(2,1)} copy(bf16[1024,2048]{0,1:T(8,128)(2,1)} %pad_maximum_fusion) | data formatting | bytes 8388608 | tf_op jit(solution)/shard_map/concatenate | solution.py:81
  115.4 7.2 %convert_element_type.40 = bf16[256,4,2048]{2,1,0:T(4,128)(2,1)} reshape(bf16[1024,2048]{1,0:T(8,128)(2,1)} %copy.36) | data formatting | bytes 8388608 | tf_op jit(solution)/shard_map/convert_element_type | solution.py:93
  122.6 10.7 %all-to-all-start = ((bf16[256,4,2048]{2,1,0:T(4,128)(2,1)}), bf16[256,4,2048]{2,1,0:T(4,128)(2,1)}, u32[]{:S(2)}, u32[]{:S(2)}) async-start(bf16[256,4,2048]{2,1,0:T(4,128)(2,1)} %convert_element_type.40), calls=%async_computation.1 | async-start | bytes 8388608 | tf_op jit(solution)/shard_map/all_to_all | solution.py:92
  133.3 0.3 reduce-scatter.2.cloned.1.call-start
  133.6 2.0 fusion.9
  135.6 0.1 copy-done.2
  135.7 0.5 fusion.11
  136.2 0.5 convolution_add_fusion
  136.8 0.5 convolution_add_fusion.1
  137.3 1.9 pad_maximum_fusion.1
  139.2 0.0 reduce-scatter.2.cloned.1.call-update
  139.2 5.8 %fusion.7 = f32[1024,256]{1,0:T(8,128)S(1)} fusion(f32[1024,1536]{1,0:T(8,128)} %fusion.13, f32[1024,1536]{1,0:T(8,128)} %copy.34, bf16[1536,1280]{1,0:T(8,128)(2,1)} %all-gather.2.cloned.1.call-done), kind=kOutput, calls=%fused_computation.15 | convolution fusion | flops 808452096 | bytes 14417920 | tf_op jit(solution)/shard_map/dot_general | solution.py:65
  145.0 1.0 slice_bitcast_fusion
  146.0 106.2 %reduce-scatter.2.cloned.1.call-done = f32[16,2560]{1,0:T(8,128)} async-done(((f32[256,2560]{1,0:T(8,128)}), f32[16,2560]{1,0:T(8,128)}) %reduce-scatter.2.cloned.1.call-update) | async-done | bytes 163856 | tf_op jit(solution)/shard_map/reduce_scatter | solution.py:83
  252.2 1.6 slice_bitcast_fusion.2
  253.8 2.3 all-to-all-done
  256.2 3.9 %convert_reduce_fusion = f32[4,2048]{1,0:T(4,128)S(1)} fusion(bf16[256,4,2048]{2,1,0:T(4,128)(2,1)} %all-to-all-done), kind=kLoop, calls=%fused_computation.1 | loop fusion | flops 4186112 | bytes 4227072 | tf_op jit(solution)/shard_map/reduce_sum | solution.py:95
  260.1 0.6 fusion.38
  (14 shorter events, 0.0 us)
Async XLA Ops:
  7.2 81.4 %all-gather.2.cloned.1.call-start = ((), (), s32[]{:S(2)}) async-start(), calls=%async_computation.2 | async-start | bytes 4177920 | tf_op jit(solution)/shard_map/all_gather | solution.py:62
  10.6 3.0 %copy-start.5 = (bf16[1,512,1536]{2,1,0:T(8,128)(2,1)S(1)}, bf16[1,512,1536]{2,1,0:T(8,128)(2,1)}, u32[]{:S(2)}) copy-start(bf16[1,512,1536]{2,1,0:T(8,128)(2,1)} %param.11) | copy-start | bytes 4718596
  14.3 3.0 %copy-start.6 = (bf16[1,512,1536]{2,1,0:T(8,128)(2,1)S(1)}, bf16[1,512,1536]{2,1,0:T(8,128)(2,1)}, u32[]{:S(2)}) copy-start(bf16[1,512,1536]{2,1,0:T(8,128)(2,1)} %param.12) | copy-start | bytes 4718596
  18.1 3.0 %copy-start.9 = (s32[1,12]{1,0:T(1,128)S(1)}, s32[1,12]{1,0:T(1,128)}, u32[]{:S(2)}) copy-start(s32[1,12]{1,0:T(1,128)} %param.13) | copy-start | bytes 148
  27.0 2.2 copy-start.3
  41.7 6.7 %copy-start.7 = (bf16[1,512,512]{2,1,0:T(8,128)(2,1)S(1)}, bf16[1,512,512]{2,1,0:T(8,128)(2,1)}, u32[]{:S(2)}) copy-start(bf16[1,512,512]{2,1,0:T(8,128)(2,1)} %param.9) | copy-start | bytes 1572868
  41.7 6.7 %copy-start.8 = (bf16[1,512,512]{2,1,0:T(8,128)(2,1)S(1)}, bf16[1,512,512]{2,1,0:T(8,128)(2,1)}, u32[]{:S(2)}) copy-start(bf16[1,512,512]{2,1,0:T(8,128)(2,1)} %param.8) | copy-start | bytes 1572868
  88.6 4.5 %copy-start = (f32[1024,1536]{1,0:T(8,128)S(1)}, f32[1024,1536]{1,0:T(8,128)}, u32[]{:S(2)}) copy-start(f32[1024,1536]{1,0:T(8,128)} %copy.34) | copy-start | bytes 18874372
  88.6 5.8 %copy-start.4 = (f32[1024,1536]{1,0:T(8,128)S(1)}, f32[1024,1536]{1,0:T(8,128)}, u32[]{:S(2)}) copy-start(f32[1024,1536]{1,0:T(8,128)} %fusion.13) | copy-start | bytes 18874372
  101.0 4.1 %copy-start.1 = (bf16[1024,1280]{1,0:T(8,128)(2,1)}, bf16[1024,1280]{1,0:T(8,128)(2,1)S(1)}, u32[]{:S(2)}) copy-start(bf16[1024,1280]{1,0:T(8,128)(2,1)S(1)} %convolution_convert_fusion) | copy-start | bytes 7864324
  122.6 133.5 %all-to-all-start = ((bf16[256,4,2048]{2,1,0:T(4,128)(2,1)}), bf16[256,4,2048]{2,1,0:T(4,128)(2,1)}, u32[]{:S(2)}, u32[]{:S(2)}) async-start(bf16[256,4,2048]{2,1,0:T(4,128)(2,1)} %convert_element_type.40), calls=%async_computation.1 | async-start | bytes 8388608 | tf_op jit(solution)/shard_map/all_to_all | solution.py:92
  133.3 118.9 %reduce-scatter.2.cloned.1.call-start = ((), (), s32[]{:S(2)}) async-start(), calls=%async_computation.3 | async-start | bytes 2785280 | tf_op jit(solution)/shard_map/reduce_scatter | solution.py:83
  133.6 2.1 copy-start.2
Sparse Core Ops, SparseCore 0:
  10.3 78.1 all-gather.1
  139.3 112.8 reduce-scatter.1

commit v2 on v1

--- a/solution.py
+++ b/solution.py
@@ -59,7 +59,9 @@
     half_work = (0.5 * product + sides).astype(jnp.bfloat16)
     full_work = (product + sides).astype(jnp.bfloat16)
     basis_rows = jnp.concatenate([mid_modes[0], mid_constraint[0]], axis=1)
-    mode_basis = lax.all_gather(basis_rows, "leaf", axis=0, tiled=True)
+    mode_basis = lax.all_to_all(
+        jnp.broadcast_to(basis_rows[None], (leaf_count,) + basis_rows.shape), "leaf", 0, 0, tiled=True
+    ).reshape(leaf_count * basis_rows.shape[0], basis_width)
     left_sum = jnp.dot(constraint, mode_basis, preferred_element_type=jnp.float32)
     right_sum = jnp.dot(half_work, mode_basis, preferred_element_type=jnp.float32)
     coupling = jnp.dot(full_work, mode_basis[:, :mode_count], preferred_element_type=jnp.float32)

time: 271 us -> 295 us (1.089)
  starting transfers between devices: 11 us -> 23.4 us
  waiting for transfers between devices: 144 us -> 155 us
    all_to_all x0 -> x1, waiting for transfers between devices: none -> 46.6 us  [body(): lax.all_to_all(jnp.broadcast_to(basis_rows[None], (leaf_count,) + basis_r...]
    all_gather x1 -> x0, waiting for transfers between devices: 35.7 us -> none  [body(): mode_basis = lax.all_gather(basis_rows, 'leaf', axis=0, tiled=True)]
    all_to_all x0 -> x1, starting transfers between devices: none -> 9.76 us  [body(): lax.all_to_all(jnp.broadcast_to(basis_rows[None], (leaf_count,) + basis_r...]
    unnamed x23 -> x25, local copies, waits for them, and re-layouts: 6.74 us -> 5.73 us
  transfers between devices with their start and end apart: 3 -> 3, of which waited for: 3 -> 3; matrix products, arithmetic and copies ran while one was open for 21% -> 19% of each run, Pallas kernels for 0% -> 0%
where the time goes in v2:
time: 295 us; the launch traced here: 291 us
  waiting for transfers between devices  155 us (53%)
  local copies, waits for them, and re-layouts  49.3 us (17%)
  matrix products  35.1 us (12%)
  starting transfers between devices  23.4 us (8%)
  other arithmetic  14.2 us (5%)
  between operations  14.2 us (5%)
    reduce_scatter x1, waiting for transfers between devices, body(): lax.psum_scatter(projected_rows(jnp.int32(0), mode_count // leaf_count *...  106 us
    all_to_all x1, waiting for transfers between devices, body(): lax.all_to_all(jnp.broadcast_to(basis_rows[None], (leaf_count,) + basis_r...  46.6 us
    all_to_all x1, starting transfers between devices, body(): lax.all_to_all(root_chunks.astype(jnp.bfloat16), ('group', 'leaf'), 0, 0,...  13.4 us
    convert_element_type x2, local copies, waits for them, and re-layouts, body(): sides = placed[leaf_order:].astype(jnp.float32)  13.2 us
    all_to_all x1, starting transfers between devices, body(): lax.all_to_all(jnp.broadcast_to(basis_rows[None], (leaf_count,) + basis_r...  9.76 us
    dot_general x8, matrix products, left_product(): lax.dot_general(first_operand, second_operand, (((0,), (0,)), ((), ())),...  9.09 us
    concatenate x3, local copies, waits for them, and re-layouts, body(): jnp.concatenate([leaf_modes[0], mass_coupling[0], damp_coupling[0]], axis=0)  9.08 us
    convert_element_type x1, local copies, waits for them, and re-layouts, body(): root_chunks.astype(jnp.bfloat16)  7.2 us
  transfers between devices with their start and end apart: 3, of which 3 were waited for; matrix products, arithmetic and copies ran while one was open for 19% of the time, Pallas kernels for 0%

profile of v2, /device:TPU:2, one launch (start us, length us, event | category | flops | bytes accessed | tf_op | source)
XLA Modules:
  0.0 291.4 jit_solution(11609662257459837441)
XLA Ops:
  7.2 0.9 pad_maximum_fusion.2
  8.1 2.3 broadcast_in_dim.19
  10.4 9.8 %all-to-all-start = ((bf16[16,96,1280]{2,1,0:T(8,128)(2,1)}), bf16[16,96,1280]{2,1,0:T(8,128)(2,1)}, u32[]{:S(2)}, u32[]{:S(2)}) async-start(bf16[16,96,1280]{2,1,0:T(8,128)(2,1)} %broadcast_in_dim.19), calls=%async_computation | async-start | bytes 7864320 | tf_op jit(solution)/shard_map/all_to_all | solution.py:62
  20.2 0.7 copy.26
  20.9 0.0 copy-start.6
  20.9 3.0 %copy.29 = bf16[512,12,128]{2,1,0:T(8,128)(2,1)} copy(bf16[512,12,128]{0,2,1:T(8,128)(2,1)S(1)} %bitcast.34) | data formatting | bytes 3145728 | tf_op jit(solution)/shard_map/concatenate | solution.py:47
  23.9 0.7 copy.27
  24.6 0.0 copy-start.7
  24.6 3.0 %copy.30 = bf16[512,12,128]{2,1,0:T(8,128)(2,1)} copy(bf16[512,12,128]{0,2,1:T(8,128)(2,1)S(1)} %bitcast.35) | data formatting | bytes 3145728 | tf_op jit(solution)/shard_map/concatenate | solution.py:47
  27.7 0.7 copy.25
  28.4 0.0 copy-start.10
  28.4 3.0 %copy.28 = bf16[512,12,128]{2,1,0:T(8,128)(2,1)} copy(bf16[512,12,128]{0,2,1:T(8,128)(2,1)S(1)} %bitcast.36) | data formatting | bytes 3145728 | tf_op jit(solution)/shard_map/concatenate | solution.py:47
  31.4 4.6 %fusion = bf16[12,1536,128]{2,0,1:T(8,128)(2,1)S(1)} fusion(bf16[512,12,128]{2,1,0:T(8,128)(2,1)} %copy.30, bf16[512,12,128]{2,1,0:T(8,128)(2,1)} %copy.29, bf16[512,12,128]{2,1,0:T(8,128)(2,1)} %copy.28, s32[12]{0:T(128)S(1)} %bitcast.43), kind=kOutput, calls=%fused_computation.2 | convolution fusion | flops 70779024 | bytes 9437232 | tf_op jit(solution)/shard_map/lbk,bj->ljk/dot_general | solution.py:9
  36.1 1.2 copy.40
  37.3 2.2 copy-done.3
  39.5 0.1 slice.74
  39.6 0.7 copy.32
  40.3 5.1 %slice_convert_fusion = f32[1024,12,128]{2,0,1:T(8,128)} fusion(bf16[1536,12,128]{2,0,1:T(8,128)(2,1)} %bitcast.33), kind=kLoop, calls=%fused_computation.16 | loop fusion | flops 1572864 | bytes 9437184 | tf_op jit(solution)/shard_map/convert_element_type | solution.py:53
  45.4 6.5 %copy.33 = f32[1024,12,128]{0,2,1:T(8,128)} copy(f32[1024,12,128]{2,0,1:T(8,128)} %slice_convert_fusion) | data formatting | bytes 12582912 | tf_op jit(solution)/shard_map/convert_element_type | solution.py:53
  52.0 6.7 %copy.34 = f32[1024,1536]{1,0:T(8,128)} copy(f32[1024,1536]{0,1:T(8,128)} %bitcast.31) | data formatting | bytes 12582912 | tf_op jit(solution)/shard_map/convert_element_type | solution.py:53
  58.7 4.5 %fusion.13 = f32[1024,1536]{1,0:T(8,128)} fusion(bf16[512,1536]{0,1:T(8,128)(2,1)S(1)} %bitcast.37, bf16[512,512]{1,0:T(8,128)(2,1)S(1)} %bitcast.41, bf16[512,512]{1,0:T(8,128)(2,1)S(1)} %bitcast.42), kind=kOutput, calls=%fused_computation.26 | convolution fusion | flops 1612709888 | bytes 8912896 | tf_op jit(solution)/shard_map/dot_general | solution.py:54
  63.1 46.6 %all-to-all-done = bf16[16,96,1280]{2,1,0:T(8,128)(2,1)} async-done(((bf16[16,96,1280]{2,1,0:T(8,128)(2,1)}), bf16[16,96,1280]{2,1,0:T(8,128)(2,1)}, u32[]{:S(2)}, u32[]{:S(2)}) %all-to-all-start) | async-done | bytes 3932192 | tf_op jit(solution)/shard_map/all_to_all | solution.py:62
  109.7 4.5 %convolution_convert_fusion.1 = bf16[512,1280]{1,0:T(8,128)(2,1)S(1)} fusion(bf16[512,1536]{0,1:T(8,128)(2,1)S(1)} %bitcast.38, bf16[1536,1280]{1,0:T(8,128)(2,1)} %bitcast.12), kind=kOutput, calls=%fused_computation.18 | convolution fusion | flops 2013921280 | bytes 6815744 | tf_op jit(solution)/shard_map/dot_general | solution.py:65
  114.3 1.2 copy-done.4
  115.5 6.6 %convolution_convert_fusion = bf16[1024,1280]{1,0:T(8,128)(2,1)S(1)} fusion(bf16[1536,1280]{1,0:T(8,128)(2,1)} %bitcast.12, f32[1024,1536]{1,0:T(8,128)S(1)} %copy-done, f32[1024,1536]{1,0:T(8,128)S(1)} %copy-done.4), kind=kOutput, calls=%fused_computation.14 | convolution fusion | flops 4032561152 | bytes 19136512 | tf_op jit(solution)/shard_map/dot_general | solution.py:66
  122.2 1.3 fusion.18
  123.5 1.3 fusion.21
  124.8 1.4 add_convert_fusion.2
  126.3 1.4 add_convert_fusion.3
  127.7 2.4 pad_maximum_fusion
  130.1 6.5 %copy.36 = bf16[1024,2048]{1,0:T(8,128)(2,1)} copy(bf16[1024,2048]{0,1:T(8,128)(2,1)} %pad_maximum_fusion) | data formatting | bytes 8388608 | tf_op jit(solution)/shard_map/concatenate | solution.py:83
  136.6 7.2 %convert_element_type.40 = bf16[256,4,2048]{2,1,0:T(4,128)(2,1)} reshape(bf16[1024,2048]{1,0:T(8,128)(2,1)} %copy.36) | data formatting | bytes 8388608 | tf_op jit(solution)/shard_map/convert_element_type | solution.py:95
  143.8 13.4 %all-to-all-start.1 = ((bf16[256,4,2048]{2,1,0:T(4,128)(2,1)}), bf16[256,4,2048]{2,1,0:T(4,128)(2,1)}, u32[]{:S(2)}, u32[]{:S(2)}) async-start(bf16[256,4,2048]{2,1,0:T(4,128)(2,1)} %convert_element_type.40), calls=%async_computation.2 | async-start | bytes 8388608 | tf_op jit(solution)/shard_map/all_to_all | solution.py:94
  157.2 0.3 reduce-scatter.2.cloned.1.call-start
  157.4 2.0 fusion.9
  159.4 0.1 copy-done.2
  159.6 0.5 fusion.11
  160.1 0.5 convolution_add_fusion
  160.6 0.5 convolution_add_fusion.1
  161.2 1.9 pad_maximum_fusion.1
  163.0 0.0 reduce-scatter.2.cloned.1.call-update
  163.0 5.8 %fusion.7 = f32[1024,256]{1,0:T(8,128)S(1)} fusion(f32[1024,1536]{1,0:T(8,128)} %fusion.13, f32[1024,1536]{1,0:T(8,128)} %copy.34, bf16[1536,1280]{1,0:T(8,128)(2,1)} %bitcast.12), kind=kOutput, calls=%fused_computation.15 | convolution fusion | flops 808452096 | bytes 14417920 | tf_op jit(solution)/shard_map/dot_general | solution.py:67
  168.8 1.0 slice_bitcast_fusion
  169.8 106.2 %reduce-scatter.2.cloned.1.call-done = f32[16,2560]{1,0:T(8,128)} async-done(((f32[256,2560]{1,0:T(8,128)}), f32[16,2560]{1,0:T(8,128)}) %reduce-scatter.2.cloned.1.call-update) | async-done | bytes 163856 | tf_op jit(solution)/shard_map/reduce_scatter | solution.py:85
  276.1 1.6 slice_bitcast_fusion.2
  277.7 2.3 all-to-all-done.1
  280.0 3.9 %convert_reduce_fusion = f32[4,2048]{1,0:T(4,128)S(1)} fusion(bf16[256,4,2048]{2,1,0:T(4,128)(2,1)} %all-to-all-done.1), kind=kLoop, calls=%fused_computation.1 | loop fusion | flops 4186112 | bytes 4227072 | tf_op jit(solution)/shard_map/reduce_sum | solution.py:97
  283.9 0.6 fusion.38
  (16 shorter events, 0.0 us)
Async XLA Ops:
  10.4 9.8 %copy-start.5 = (bf16[1,512,1536]{2,1,0:T(8,128)(2,1)S(1)}, bf16[1,512,1536]{2,1,0:T(8,128)(2,1)}, u32[]{:S(2)}) copy-start(bf16[1,512,1536]{2,1,0:T(8,128)(2,1)} %param.10) | copy-start | bytes 4718596
  10.4 99.4 %all-to-all-start = ((bf16[16,96,1280]{2,1,0:T(8,128)(2,1)}), bf16[16,96,1280]{2,1,0:T(8,128)(2,1)}, u32[]{:S(2)}, u32[]{:S(2)}) async-start(bf16[16,96,1280]{2,1,0:T(8,128)(2,1)} %broadcast_in_dim.19), calls=%async_computation | async-start | bytes 7864320 | tf_op jit(solution)/shard_map/all_to_all | solution.py:62
  20.9 3.0 %copy-start.6 = (bf16[1,512,1536]{2,1,0:T(8,128)(2,1)S(1)}, bf16[1,512,1536]{2,1,0:T(8,128)(2,1)}, u32[]{:S(2)}) copy-start(bf16[1,512,1536]{2,1,0:T(8,128)(2,1)} %param.11) | copy-start | bytes 4718596
  24.6 3.0 %copy-start.7 = (bf16[1,512,1536]{2,1,0:T(8,128)(2,1)S(1)}, bf16[1,512,1536]{2,1,0:T(8,128)(2,1)}, u32[]{:S(2)}) copy-start(bf16[1,512,1536]{2,1,0:T(8,128)(2,1)} %param.12) | copy-start | bytes 4718596
  28.4 3.0 %copy-start.10 = (s32[1,12]{1,0:T(1,128)S(1)}, s32[1,12]{1,0:T(1,128)}, u32[]{:S(2)}) copy-start(s32[1,12]{1,0:T(1,128)} %param.13) | copy-start | bytes 148
  37.3 2.2 copy-start.3
  52.0 6.7 %copy-start.8 = (bf16[1,512,512]{2,1,0:T(8,128)(2,1)S(1)}, bf16[1,512,512]{2,1,0:T(8,128)(2,1)}, u32[]{:S(2)}) copy-start(bf16[1,512,512]{2,1,0:T(8,128)(2,1)} %param.9) | copy-start | bytes 1572868
  52.0 6.7 %copy-start.9 = (bf16[1,512,512]{2,1,0:T(8,128)(2,1)S(1)}, bf16[1,512,512]{2,1,0:T(8,128)(2,1)}, u32[]{:S(2)}) copy-start(bf16[1,512,512]{2,1,0:T(8,128)(2,1)} %param.8) | copy-start | bytes 1572868
  109.7 4.5 %copy-start = (f32[1024,1536]{1,0:T(8,128)S(1)}, f32[1024,1536]{1,0:T(8,128)}, u32[]{:S(2)}) copy-start(f32[1024,1536]{1,0:T(8,128)} %copy.34) | copy-start | bytes 18874372
  109.7 5.8 %copy-start.4 = (f32[1024,1536]{1,0:T(8,128)S(1)}, f32[1024,1536]{1,0:T(8,128)}, u32[]{:S(2)}) copy-start(f32[1024,1536]{1,0:T(8,128)} %fusion.13) | copy-start | bytes 18874372
  122.1 4.1 %copy-start.1 = (bf16[1024,1280]{1,0:T(8,128)(2,1)}, bf16[1024,1280]{1,0:T(8,128)(2,1)S(1)}, u32[]{:S(2)}) copy-start(bf16[1024,1280]{1,0:T(8,128)(2,1)S(1)} %convolution_convert_fusion) | copy-start | bytes 7864324
  143.8 136.2 %all-to-all-start.1 = ((bf16[256,4,2048]{2,1,0:T(4,128)(2,1)}), bf16[256,4,2048]{2,1,0:T(4,128)(2,1)}, u32[]{:S(2)}, u32[]{:S(2)}) async-start(bf16[256,4,2048]{2,1,0:T(4,128)(2,1)} %convert_element_type.40), calls=%async_computation.2 | async-start | bytes 8388608 | tf_op jit(solution)/shard_map/all_to_all | solution.py:94
  157.2 118.9 %reduce-scatter.2.cloned.1.call-start = ((), (), s32[]{:S(2)}) async-start(), calls=%async_computation.3 | async-start | bytes 2785280 | tf_op jit(solution)/shard_map/reduce_scatter | solution.py:85
  157.4 2.1 copy-start.2
Sparse Core Ops, SparseCore 0:
  163.2 112.8 reduce-scatter.1

commit v3 on v1

--- a/solution.py
+++ b/solution.py
@@ -80,11 +80,17 @@
         )
         return jnp.concatenate([mass_term, damp_term], axis=1)
 
-    modal_part = lax.psum_scatter(
-        projected_rows(jnp.int32(0), mode_count // leaf_count * lax.axis_size("leaf"), 0),
+    modal_rows = projected_rows(jnp.int32(0), mode_count, 0)
+    modal_recv = lax.all_to_all(
+        modal_rows.reshape(leaf_count, mode_count // leaf_count, 2 * basis_width).astype(jnp.bfloat16),
         "leaf",
-        scatter_dimension=0,
+        0,
+        0,
         tiled=True,
+    )
+    modal_part = jnp.sum(
+        modal_recv.reshape(leaf_count, mode_count // leaf_count, 2 * basis_width).astype(jnp.float32),
+        axis=0,
     )
     root_rows = projected_rows(jnp.int32(0) + mode_count, root_width, mode_count)
     device_count = group_count * leaf_count

time: 271 us -> 256 us (0.945)
  waiting for transfers between devices: 144 us -> 125 us
  starting transfers between devices: 11 us -> 18.5 us
    reduce_scatter x1 -> x0, waiting for transfers between devices: 106 us -> none  [body(): lax.psum_scatter(projected_rows(jnp.int32(0), mode_count // leaf_count *...]
    all_to_all x1, waiting for transfers between devices: 2.35 us -> 88.9 us  [body(): lax.all_to_all(root_chunks.astype(jnp.bfloat16), ('group', 'leaf'), 0, 0,...]
    all_to_all x0 -> x1, starting transfers between devices: none -> 4.55 us  [body(): lax.all_to_all(modal_rows.reshape(leaf_count, mode_count // leaf_count, 2...]
    all_to_all x1, starting transfers between devices: 10.7 us -> 13.9 us  [body(): lax.all_to_all(root_chunks.astype(jnp.bfloat16), ('group', 'leaf'), 0, 0,...]
  transfers between devices with their start and end apart: 3 -> 3, of which waited for: 3 -> 2; matrix products, arithmetic and copies ran while one was open for 21% -> 28% of each run, Pallas kernels for 0% -> 0%
where the time goes in v3:
time: 256 us; the launch traced here: 254 us
  waiting for transfers between devices  125 us (49%)
  local copies, waits for them, and re-layouts  47 us (18%)
  matrix products  35 us (14%)
  starting transfers between devices  18.5 us (7%)
  other arithmetic  14.5 us (6%)
  between operations  14.2 us (6%)
    all_to_all x1, waiting for transfers between devices, body(): lax.all_to_all(root_chunks.astype(jnp.bfloat16), ('group', 'leaf'), 0, 0,...  88.9 us
    all_gather x1, waiting for transfers between devices, body(): mode_basis = lax.all_gather(basis_rows, 'leaf', axis=0, tiled=True)  35.7 us
    all_to_all x1, starting transfers between devices, body(): lax.all_to_all(root_chunks.astype(jnp.bfloat16), ('group', 'leaf'), 0, 0,...  13.9 us
    convert_element_type x2, local copies, waits for them, and re-layouts, body(): sides = placed[leaf_order:].astype(jnp.float32)  13.3 us
    dot_general x8, matrix products, left_product(): lax.dot_general(first_operand, second_operand, (((0,), (0,)), ((), ())),...  9.03 us
    concatenate x3, local copies, waits for them, and re-layouts, body(): jnp.concatenate([leaf_modes[0], mass_coupling[0], damp_coupling[0]], axis=0)  9.02 us
    convert_element_type x1, local copies, waits for them, and re-layouts, body(): root_chunks.astype(jnp.bfloat16)  7.19 us
    unnamed x23, local copies, waits for them, and re-layouts  6.62 us
  transfers between devices with their start and end apart: 3, of which 2 were waited for; matrix products, arithmetic and copies ran while one was open for 28% of the time, Pallas kernels for 0%

profile of v3, /device:TPU:2, one launch (start us, length us, event | category | flops | bytes accessed | tf_op | source)
XLA Modules:
  0.0 253.8 jit_solution(8917956974490837239)
XLA Ops:
  7.2 0.0 all-gather.2.cloned.1.call-start
  7.2 1.6 pad_maximum_fusion.2
  8.9 0.0 all-gather.2.cloned.1.call-update
  8.9 1.7 copy.26
  10.6 0.0 copy-start.5
  10.6 3.0 %copy.29 = bf16[512,12,128]{2,1,0:T(8,128)(2,1)} copy(bf16[512,12,128]{0,2,1:T(8,128)(2,1)S(1)} %bitcast.34) | data formatting | bytes 3145728 | tf_op jit(solution)/shard_map/concatenate | solution.py:47
  13.6 0.0 copy-done.5
  13.6 0.7 copy.27
  14.3 0.0 copy-start.6
  14.3 3.0 %copy.30 = bf16[512,12,128]{2,1,0:T(8,128)(2,1)} copy(bf16[512,12,128]{0,2,1:T(8,128)(2,1)S(1)} %bitcast.35) | data formatting | bytes 3145728 | tf_op jit(solution)/shard_map/concatenate | solution.py:47
  17.3 0.7 copy.25
  18.0 0.0 copy-start.9
  18.1 3.0 %copy.28 = bf16[512,12,128]{2,1,0:T(8,128)(2,1)} copy(bf16[512,12,128]{0,2,1:T(8,128)(2,1)S(1)} %bitcast.36) | data formatting | bytes 3145728 | tf_op jit(solution)/shard_map/concatenate | solution.py:47
  21.1 4.6 %fusion = bf16[12,1536,128]{2,0,1:T(8,128)(2,1)S(1)} fusion(bf16[512,12,128]{2,1,0:T(8,128)(2,1)} %copy.30, bf16[512,12,128]{2,1,0:T(8,128)(2,1)} %copy.29, bf16[512,12,128]{2,1,0:T(8,128)(2,1)} %copy.28, s32[12]{0:T(128)S(1)} %bitcast.44), kind=kOutput, calls=%fused_computation.2 | convolution fusion | flops 70779024 | bytes 9437232 | tf_op jit(solution)/shard_map/lbk,bj->ljk/dot_general | solution.py:9
  25.7 1.2 copy.40
  27.0 2.2 copy-done.3
  29.2 0.1 slice.74
  29.3 0.7 copy.32
  30.0 5.1 %slice_convert_fusion = f32[1024,12,128]{2,0,1:T(8,128)} fusion(bf16[1536,12,128]{2,0,1:T(8,128)(2,1)} %bitcast.33), kind=kLoop, calls=%fused_computation.16 | loop fusion | flops 1572864 | bytes 9437184 | tf_op jit(solution)/shard_map/convert_element_type | solution.py:53
  35.1 6.6 %copy.33 = f32[1024,12,128]{0,2,1:T(8,128)} copy(f32[1024,12,128]{2,0,1:T(8,128)} %slice_convert_fusion) | data formatting | bytes 12582912 | tf_op jit(solution)/shard_map/convert_element_type | solution.py:53
  41.7 6.7 %copy.34 = f32[1024,1536]{1,0:T(8,128)} copy(f32[1024,1536]{0,1:T(8,128)} %bitcast.31) | data formatting | bytes 12582912 | tf_op jit(solution)/shard_map/convert_element_type | solution.py:53
  48.4 4.5 %fusion.15 = f32[1024,1536]{1,0:T(8,128)} fusion(bf16[512,1536]{0,1:T(8,128)(2,1)S(1)} %bitcast.38, bf16[512,512]{1,0:T(8,128)(2,1)S(1)} %bitcast.42, bf16[512,512]{1,0:T(8,128)(2,1)S(1)} %bitcast.43), kind=kOutput, calls=%fused_computation.29 | convolution fusion | flops 1612709888 | bytes 8912896 | tf_op jit(solution)/shard_map/dot_general | solution.py:54
  52.9 35.7 %all-gather.2.cloned.1.call-done = bf16[1536,1280]{1,0:T(8,128)(2,1)} async-done(((bf16[96,1280]{1,0:T(8,128)(2,1)}), bf16[1536,1280]{1,0:T(8,128)(2,1)}) %all-gather.2.cloned.1.call-update) | async-done | bytes 3932176 | tf_op jit(solution)/shard_map/all_gather | solution.py:62
  88.6 4.5 %convolution_convert_fusion.1 = bf16[512,1280]{1,0:T(8,128)(2,1)S(1)} fusion(bf16[512,1536]{0,1:T(8,128)(2,1)S(1)} %bitcast.39, bf16[1536,1280]{1,0:T(8,128)(2,1)} %all-gather.2.cloned.1.call-done), kind=kOutput, calls=%fused_computation.18 | convolution fusion | flops 2013921280 | bytes 6815744 | tf_op jit(solution)/shard_map/dot_general | solution.py:63
  93.1 1.3 copy-done.4
  94.4 6.6 %convolution_convert_fusion = bf16[1024,1280]{1,0:T(8,128)(2,1)S(1)} fusion(bf16[1536,1280]{1,0:T(8,128)(2,1)} %all-gather.2.cloned.1.call-done, f32[1024,1536]{1,0:T(8,128)S(1)} %copy-done, f32[1024,1536]{1,0:T(8,128)S(1)} %copy-done.4), kind=kOutput, calls=%fused_computation.14 | convolution fusion | flops 4032561152 | bytes 19136512 | tf_op jit(solution)/shard_map/dot_general | solution.py:64
  101.0 0.5 fusion.11
  101.5 0.5 fusion.13
  102.1 0.5 fusion.10
  102.6 0.5 fusion.9
  103.1 1.3 pad_maximum_fusion.1
  104.4 4.6 %all-to-all-start = ((bf16[16,16,2560]{2,1,0:T(8,128)(2,1)}), bf16[16,16,2560]{2,1,0:T(8,128)(2,1)S(1)}, u32[]{:S(2)}, u32[]{:S(2)}) async-start(bf16[16,16,2560]{2,1,0:T(8,128)(2,1)} %bitcast.37), calls=%async_computation | async-start | bytes 2621440 | tf_op jit(solution)/shard_map/all_to_all | solution.py:84
  109.0 2.7 %fusion.20 = f32[1024,1024]{0,1:T(8,128)S(1)} fusion(bf16[1024,1280]{1,0:T(8,128)(2,1)} %copy-done.1, bf16[512,1280]{1,0:T(8,128)(2,1)S(1)} %convolution_convert_fusion.1), kind=kOutput, calls=%fused_computation.34 | convolution fusion | flops 1073741824 | bytes 6291456 | tf_op jit(solution)/shard_map/dot_general | solution.py:19
  111.7 1.3 fusion.23
  113.0 1.4 add_convert_fusion.2
  114.5 1.4 add_convert_fusion.3
  115.9 2.4 pad_maximum_fusion
  118.3 6.5 %copy.36 = bf16[1024,2048]{1,0:T(8,128)(2,1)} copy(bf16[1024,2048]{0,1:T(8,128)(2,1)} %pad_maximum_fusion) | data formatting | bytes 8388608 | tf_op jit(solution)/shard_map/concatenate | solution.py:81
  124.8 7.2 %convert_element_type.49 = bf16[256,4,2048]{2,1,0:T(4,128)(2,1)} reshape(bf16[1024,2048]{1,0:T(8,128)(2,1)} %copy.36) | data formatting | bytes 8388608 | tf_op jit(solution)/shard_map/convert_element_type | solution.py:99
  132.0 0.0 all-to-all-done
  132.0 13.9 %all-to-all-start.1 = ((bf16[256,4,2048]{2,1,0:T(4,128)(2,1)}), bf16[256,4,2048]{2,1,0:T(4,128)(2,1)}, u32[]{:S(2)}, u32[]{:S(2)}) async-start(bf16[256,4,2048]{2,1,0:T(4,128)(2,1)} %convert_element_type.49), calls=%async_computation.1 | async-start | bytes 8388608 | tf_op jit(solution)/shard_map/all_to_all | solution.py:98
  145.9 5.7 %fusion.7 = f32[1024,256]{1,0:T(8,128)S(1)} fusion(f32[1024,1536]{1,0:T(8,128)} %fusion.15, f32[1024,1536]{1,0:T(8,128)} %copy.34, bf16[1536,1280]{1,0:T(8,128)(2,1)} %all-gather.2.cloned.1.call-done), kind=kOutput, calls=%fused_computation.15 | convolution fusion | flops 808452096 | bytes 14417920 | tf_op jit(solution)/shard_map/dot_general | solution.py:65
  151.6 1.0 slice_bitcast_fusion
  152.7 0.2 convert_reduce_fusion.1
  152.9 0.7 slice_bitcast_fusion.2
  153.5 88.9 %all-to-all-done.1 = bf16[256,4,2048]{2,1,0:T(4,128)(2,1)} async-done(((bf16[256,4,2048]{2,1,0:T(4,128)(2,1)}), bf16[256,4,2048]{2,1,0:T(4,128)(2,1)}, u32[]{:S(2)}, u32[]{:S(2)}) %all-to-all-start.1) | async-done | bytes 4194336 | tf_op jit(solution)/shard_map/all_to_all | solution.py:98
  242.5 3.9 %convert_reduce_fusion = f32[4,2048]{1,0:T(4,128)S(1)} fusion(bf16[256,4,2048]{2,1,0:T(4,128)(2,1)} %all-to-all-done.1), kind=kLoop, calls=%fused_computation.1 | loop fusion | flops 4186112 | bytes 4227072 | tf_op jit(solution)/shard_map/reduce_sum | solution.py:101
  246.4 0.6 fusion.40
  (14 shorter events, 0.0 us)
Async XLA Ops:
  7.2 81.4 %all-gather.2.cloned.1.call-start = ((), (), s32[]{:S(2)}) async-start(), calls=%async_computation.2 | async-start | bytes 4177920 | tf_op jit(solution)/shard_map/all_gather | solution.py:62
  10.6 3.0 %copy-start.5 = (bf16[1,512,1536]{2,1,0:T(8,128)(2,1)S(1)}, bf16[1,512,1536]{2,1,0:T(8,128)(2,1)}, u32[]{:S(2)}) copy-start(bf16[1,512,1536]{2,1,0:T(8,128)(2,1)} %param.11) | copy-start | bytes 4718596
  14.3 3.0 %copy-start.6 = (bf16[1,512,1536]{2,1,0:T(8,128)(2,1)S(1)}, bf16[1,512,1536]{2,1,0:T(8,128)(2,1)}, u32[]{:S(2)}) copy-start(bf16[1,512,1536]{2,1,0:T(8,128)(2,1)} %param.12) | copy-start | bytes 4718596
  18.0 3.0 %copy-start.9 = (s32[1,12]{1,0:T(1,128)S(1)}, s32[1,12]{1,0:T(1,128)}, u32[]{:S(2)}) copy-start(s32[1,12]{1,0:T(1,128)} %param.13) | copy-start | bytes 148
  26.9 2.2 copy-start.3
  41.7 6.7 %copy-start.7 = (bf16[1,512,512]{2,1,0:T(8,128)(2,1)S(1)}, bf16[1,512,512]{2,1,0:T(8,128)(2,1)}, u32[]{:S(2)}) copy-start(bf16[1,512,512]{2,1,0:T(8,128)(2,1)} %param.9) | copy-start | bytes 1572868
  41.7 6.7 %copy-start.8 = (bf16[1,512,512]{2,1,0:T(8,128)(2,1)S(1)}, bf16[1,512,512]{2,1,0:T(8,128)(2,1)}, u32[]{:S(2)}) copy-start(bf16[1,512,512]{2,1,0:T(8,128)(2,1)} %param.8) | copy-start | bytes 1572868
  88.6 4.5 %copy-start = (f32[1024,1536]{1,0:T(8,128)S(1)}, f32[1024,1536]{1,0:T(8,128)}, u32[]{:S(2)}) copy-start(f32[1024,1536]{1,0:T(8,128)} %copy.34) | copy-start | bytes 18874372
  88.6 5.8 %copy-start.4 = (f32[1024,1536]{1,0:T(8,128)S(1)}, f32[1024,1536]{1,0:T(8,128)}, u32[]{:S(2)}) copy-start(f32[1024,1536]{1,0:T(8,128)} %fusion.15) | copy-start | bytes 18874372
  101.0 1.6 copy-start.1
  104.4 27.6 %all-to-all-start = ((bf16[16,16,2560]{2,1,0:T(8,128)(2,1)}), bf16[16,16,2560]{2,1,0:T(8,128)(2,1)S(1)}, u32[]{:S(2)}, u32[]{:S(2)}) async-start(bf16[16,16,2560]{2,1,0:T(8,128)(2,1)} %bitcast.37), calls=%async_computation | async-start | bytes 2621440 | tf_op jit(solution)/shard_map/all_to_all | solution.py:84
  109.0 2.7 %copy-start.2 = (bf16[1024,1280]{1,0:T(8,128)(2,1)S(1)}, bf16[1024,1280]{1,0:T(8,128)(2,1)}, u32[]{:S(2)}) copy-start(bf16[1024,1280]{1,0:T(8,128)(2,1)} %copy-done.1) | copy-start | bytes 7864324
  132.0 110.5 %all-to-all-start.1 = ((bf16[256,4,2048]{2,1,0:T(4,128)(2,1)}), bf16[256,4,2048]{2,1,0:T(4,128)(2,1)}, u32[]{:S(2)}, u32[]{:S(2)}) async-start(bf16[256,4,2048]{2,1,0:T(4,128)(2,1)} %convert_element_type.49), calls=%async_computation.1 | async-start | bytes 8388608 | tf_op jit(solution)/shard_map/all_to_all | solution.py:98
Sparse Core Ops, SparseCore 0:
  10.3 78.1 all-gather.1

commit v4 on v3

--- a/solution.py
+++ b/solution.py
@@ -92,23 +92,41 @@
         modal_recv.reshape(leaf_count, mode_count // leaf_count, 2 * basis_width).astype(jnp.float32),
         axis=0,
     )
-    root_rows = projected_rows(jnp.int32(0) + mode_count, root_width, mode_count)
     device_count = group_count * leaf_count
-    root_chunks = root_rows.reshape(device_count, root_width // device_count, 2 * root_width)
+    core_odd = lax.axis_index("group") % 2 == 1
+    left_root = left_part[:, mode_count:]
+    mass_root = right_mass[:, mode_count:]
+    damp_root = right_damp[:, mode_count:]
+    own_right = jnp.where(core_odd, damp_root, mass_root)
+    other_right = jnp.where(core_odd, mass_root, damp_root)
+    partner = lax.ppermute(
+        jnp.concatenate([left_root, other_right], axis=0),
+        "group",
+        [(index, index ^ 1) for index in range(group_count)],
+    )
+    left_pair = jnp.concatenate([left_root, partner[:leaf_order]], axis=0)
+    right_pair = jnp.concatenate([own_right, partner[leaf_order:]], axis=0)
+    root_rows = left_product(left_pair, right_pair) + left_product(right_pair, left_pair)
     root_recv = lax.all_to_all(
-        root_chunks.astype(jnp.bfloat16), ("group", "leaf"), 0, 0, tiled=True
+        root_rows.reshape(device_count, root_width // device_count, root_width).astype(jnp.bfloat16),
+        ("group", "leaf"),
+        0,
+        0,
+        tiled=True,
     )
     root_part = jnp.sum(
-        root_recv.reshape(device_count, root_width // device_count, 2 * root_width).astype(jnp.float32),
-        axis=0,
+        root_recv.reshape(
+            group_count // 2, 2, leaf_count, root_width // device_count, root_width
+        ).astype(jnp.float32),
+        axis=(0, 2),
     )
     return (
         coupling[:leaf_order][None],
         coupling[leaf_order:][None],
         modal_part[:, :basis_width][None],
         modal_part[:, basis_width:][None],
-        root_part[:, :root_width],
-        root_part[:, root_width:],
+        root_part[0],
+        root_part[1],
     )
 
 

time: 256 us -> 218 us (0.85)
  waiting for transfers between devices: 125 us -> 103 us
  local copies, waits for them, and re-layouts: 47 us -> 39.1 us
  starting transfers between devices: 18.5 us -> 13.2 us
  other arithmetic: 14.5 us -> 10.7 us
    all_to_all x1, waiting for transfers between devices: 88.9 us -> 44.9 us  [body(): lax.all_to_all(root_rows.reshape(device_count, root_width // device_count...]
    all_to_all x1, waiting for transfers between devices: 0.01 us -> 21.6 us  [body(): lax.all_to_all(modal_rows.reshape(leaf_count, mode_count // leaf_count, 2...]
    concatenate x1 -> x0, local copies, waits for them, and re-layouts: 6.54 us -> none  [projected_rows(): return jnp.concatenate([mass_term, damp_term], axis=1)]
    all_to_all x1, starting transfers between devices: 13.9 us -> 9.3 us  [body(): lax.all_to_all(root_rows.reshape(device_count, root_width // device_count...]
    convert_element_type x1, local copies, waits for them, and re-layouts: 7.19 us -> 4.12 us  [body(): root_rows.reshape(device_count, root_width // device_count, root_width)]
    reduce_sum x1, other arithmetic: 3.9 us -> 0.84 us  [body(): jnp.sum(root_recv.reshape(group_count // 2, 2, leaf_count, root_width //...]
    dot_general x8 -> x6, matrix products: 9.03 us -> 8.37 us  [left_product(): lax.dot_general(first_operand, second_operand, (((0,), (0,)), ((), ())),...]
    unnamed x23 -> x19, local copies, waits for them, and re-layouts: 6.62 us -> 6.47 us
  transfers between devices with their start and end apart: 3 -> 4, of which waited for: 2 -> 3; matrix products, arithmetic and copies ran while one was open for 28% -> 30% of each run, Pallas kernels for 0% -> 0%
where the time goes in v4:
time: 218 us; the launch traced here: 214 us
  waiting for transfers between devices  103 us (47%)
  local copies, waits for them, and re-layouts  39.1 us (18%)
  matrix products  34.3 us (16%)
  between operations  14.2 us (7%)
  starting transfers between devices  13.2 us (6%)
  other arithmetic  10.7 us (5%)
    all_to_all x1, waiting for transfers between devices, body(): lax.all_to_all(root_rows.reshape(device_count, root_width // device_count...  44.9 us
    all_gather x1, waiting for transfers between devices, body(): mode_basis = lax.all_gather(basis_rows, 'leaf', axis=0, tiled=True)  36.4 us
    all_to_all x1, waiting for transfers between devices, body(): lax.all_to_all(modal_rows.reshape(leaf_count, mode_count // leaf_count, 2...  21.6 us
    convert_element_type x2, local copies, waits for them, and re-layouts, body(): sides = placed[leaf_order:].astype(jnp.float32)  13.3 us
    all_to_all x1, starting transfers between devices, body(): lax.all_to_all(root_rows.reshape(device_count, root_width // device_count...  9.3 us
    concatenate x3, local copies, waits for them, and re-layouts, body(): jnp.concatenate([leaf_modes[0], mass_coupling[0], damp_coupling[0]], axis=0)  9.04 us
    dot_general x6, matrix products, left_product(): lax.dot_general(first_operand, second_operand, (((0,), (0,)), ((), ())),...  8.37 us
    dot_general x1, matrix products, body(): jnp.dot(half_work, mode_basis, preferred_element_type=jnp.float32)  6.6 us
  transfers between devices with their start and end apart: 4, of which 3 were waited for; matrix products, arithmetic and copies ran while one was open for 30% of the time, Pallas kernels for 0%

profile of v4, /device:TPU:2, one launch (start us, length us, event | category | flops | bytes accessed | tf_op | source)
XLA Modules:
  0.0 214.5 jit_solution(11552914401208624062)
XLA Ops:
  7.2 0.0 all-gather.2.cloned.1.call-start
  7.2 1.6 pad_maximum_fusion.8
  8.9 0.0 all-gather.2.cloned.1.call-update
  8.9 1.7 copy.26
  10.6 0.0 copy-start.3
  10.6 3.0 %copy.29 = bf16[512,12,128]{2,1,0:T(8,128)(2,1)} copy(bf16[512,12,128]{0,2,1:T(8,128)(2,1)S(1)} %bitcast.41) | data formatting | bytes 3145728 | tf_op jit(solution)/shard_map/concatenate | solution.py:47
  13.6 0.7 copy.25
  14.3 0.0 copy-start.4
  14.4 3.0 %copy.28 = bf16[512,12,128]{2,1,0:T(8,128)(2,1)} copy(bf16[512,12,128]{0,2,1:T(8,128)(2,1)S(1)} %bitcast.42) | data formatting | bytes 3145728 | tf_op jit(solution)/shard_map/concatenate | solution.py:47
  17.4 0.7 copy.24
  18.1 0.0 copy-start.7
  18.1 3.0 %copy.27 = bf16[512,12,128]{2,1,0:T(8,128)(2,1)} copy(bf16[512,12,128]{0,2,1:T(8,128)(2,1)S(1)} %bitcast.43) | data formatting | bytes 3145728 | tf_op jit(solution)/shard_map/concatenate | solution.py:47
  21.1 4.6 %fusion = bf16[12,1536,128]{2,0,1:T(8,128)(2,1)S(1)} fusion(bf16[512,12,128]{2,1,0:T(8,128)(2,1)} %copy.29, bf16[512,12,128]{2,1,0:T(8,128)(2,1)} %copy.28, bf16[512,12,128]{2,1,0:T(8,128)(2,1)} %copy.27, s32[12]{0:T(128)S(1)} %bitcast.50), kind=kOutput, calls=%fused_computation.1 | convolution fusion | flops 70779024 | bytes 9437232 | tf_op jit(solution)/shard_map/lbk,bj->ljk/dot_general | solution.py:9
  25.7 1.2 copy.38
  27.0 2.2 %copy-done.1 = bf16[12,1536,128]{2,1,0:T(8,128)(2,1)} copy-done((bf16[12,1536,128]{2,1,0:T(8,128)(2,1)}, bf16[12,1536,128]{2,1,0:T(8,128)(2,1)S(1)}, u32[]{:S(2)}) %copy-start.1) | copy-done | bytes 4718616
  29.2 0.1 slice.81
  29.3 0.7 copy.31
  30.0 5.1 %slice_convert_fusion = f32[1024,12,128]{2,0,1:T(8,128)} fusion(bf16[1536,12,128]{2,0,1:T(8,128)(2,1)} %bitcast.39), kind=kLoop, calls=%fused_computation.14 | loop fusion | flops 1572864 | bytes 9437184 | tf_op jit(solution)/shard_map/convert_element_type | solution.py:53
  35.1 6.6 %copy.32 = f32[1024,12,128]{0,2,1:T(8,128)} copy(f32[1024,12,128]{2,0,1:T(8,128)} %slice_convert_fusion) | data formatting | bytes 12582912 | tf_op jit(solution)/shard_map/convert_element_type | solution.py:53
  41.7 6.7 %copy.33 = f32[1024,1536]{1,0:T(8,128)} copy(f32[1024,1536]{0,1:T(8,128)} %bitcast.37) | data formatting | bytes 12582912 | tf_op jit(solution)/shard_map/convert_element_type | solution.py:53
  48.4 4.5 %fusion.16 = f32[1024,1536]{1,0:T(8,128)} fusion(bf16[512,1536]{0,1:T(8,128)(2,1)S(1)} %bitcast.44, bf16[512,512]{1,0:T(8,128)(2,1)S(1)} %bitcast.48, bf16[512,512]{1,0:T(8,128)(2,1)S(1)} %bitcast.49), kind=kOutput, calls=%fused_computation.31 | convolution fusion | flops 1612709888 | bytes 8912896 | tf_op jit(solution)/shard_map/dot_general | solution.py:54
  52.9 36.4 %all-gather.2.cloned.1.call-done = bf16[1536,1280]{1,0:T(8,128)(2,1)} async-done(((bf16[96,1280]{1,0:T(8,128)(2,1)}), bf16[1536,1280]{1,0:T(8,128)(2,1)}) %all-gather.2.cloned.1.call-update) | async-done | bytes 3932176 | tf_op jit(solution)/shard_map/all_gather | solution.py:62
  89.4 4.5 %convolution_convert_fusion.1 = bf16[512,1280]{1,0:T(8,128)(2,1)S(1)} fusion(bf16[512,1536]{0,1:T(8,128)(2,1)S(1)} %bitcast.45, bf16[1536,1280]{1,0:T(8,128)(2,1)} %all-gather.2.cloned.1.call-done), kind=kOutput, calls=%fused_computation.16 | convolution fusion | flops 2013921280 | bytes 6815744 | tf_op jit(solution)/shard_map/dot_general | solution.py:63
  93.9 0.1 slice.92
  94.0 1.1 copy-done.2
  95.1 6.6 %convolution_convert_fusion = bf16[1024,1280]{1,0:T(8,128)(2,1)S(1)} fusion(bf16[1536,1280]{1,0:T(8,128)(2,1)} %all-gather.2.cloned.1.call-done, f32[1024,1536]{1,0:T(8,128)S(1)} %copy-done, f32[1024,1536]{1,0:T(8,128)S(1)} %copy-done.2), kind=kOutput, calls=%fused_computation.12 | convolution fusion | flops 4032561152 | bytes 19136512 | tf_op jit(solution)/shard_map/dot_general | solution.py:64
  101.8 0.5 fusion.12
  102.3 0.5 fusion.10
  102.8 0.1 broadcast_select_fusion
  103.0 1.6 pad_maximum_fusion
  104.6 0.5 fusion.14
  105.1 0.5 fusion.9
  105.7 1.1 pad_maximum_fusion.7
  106.8 3.9 %all-to-all-start = ((bf16[16,16,2560]{2,1,0:T(8,128)(2,1)}), bf16[16,16,2560]{2,1,0:T(8,128)(2,1)S(1)}, u32[]{:S(2)}, u32[]{:S(2)}) async-start(bf16[16,16,2560]{2,1,0:T(8,128)(2,1)} %bitcast.14), calls=%async_computation | async-start | bytes 2621440 | tf_op jit(solution)/shard_map/all_to_all | solution.py:84
  110.7 0.0 collective-permute-done
  110.7 1.7 fusion.33
  112.4 2.4 %fusion.11 = f32[1024,1024]{1,0:T(8,128)S(1)} fusion(bf16[512,1024]{1,0:T(8,128)(2,1)S(1)} %get-tuple-element.9, bf16[512,1024]{1,0:T(8,128)(2,1)S(1)} %get-tuple-element.6, bf16[512,1024]{1,0:T(8,128)(2,1)S(1)} %slice.92, bf16[512,1024]{1,0:T(8,128)(2,1)S(1)} %get-tuple-element.8), kind=kOutput, calls=%fused_computation.25 | convolution fusion | flops 2155872256 | bytes 8388608 | tf_op jit(solution)/shard_map/dot_general | solution.py:19
  114.8 3.8 %add_convert_fusion.2 = bf16[1024,1024]{1,0:T(8,128)(2,1)} fusion(f32[1024,1024]{1,0:T(8,128)S(1)} %fusion.11, bf16[512,1024]{1,0:T(8,128)(2,1)S(1)} %get-tuple-element.9, bf16[512,1024]{1,0:T(8,128)(2,1)S(1)} %get-tuple-element.6, bf16[512,1024]{1,0:T(8,128)(2,1)S(1)} %slice.92, bf16[512,1024]{1,0:T(8,128)(2,1)S(1)} %get-tuple-element.8), kind=kOutput, calls=%fused_computation.11 | convolution fusion | flops 2157969408 | bytes 10485760 | tf_op jit(solution)/shard_map/dot_general | solution.py:19
  118.7 4.1 %convert_element_type.55 = bf16[256,4,1024]{2,1,0:T(4,128)(2,1)} reshape(bf16[1024,1024]{1,0:T(8,128)(2,1)} %add_convert_fusion.2) | data formatting | bytes 4194304 | tf_op jit(solution)/shard_map/convert_element_type | solution.py:111
  122.8 21.6 %all-to-all-done = bf16[16,16,2560]{2,1,0:T(8,128)(2,1)S(1)} async-done(((bf16[16,16,2560]{2,1,0:T(8,128)(2,1)}), bf16[16,16,2560]{2,1,0:T(8,128)(2,1)S(1)}, u32[]{:S(2)}, u32[]{:S(2)}) %all-to-all-start) | async-done | bytes 1310752 | tf_op jit(solution)/shard_map/all_to_all | solution.py:84
  144.4 9.3 %all-to-all-start.1 = ((bf16[256,4,1024]{2,1,0:T(4,128)(2,1)}), bf16[256,4,1024]{2,1,0:T(4,128)(2,1)S(1)}, u32[]{:S(2)}, u32[]{:S(2)}) async-start(bf16[256,4,1024]{2,1,0:T(4,128)(2,1)} %convert_element_type.55), calls=%async_computation.1 | async-start | bytes 4194304 | tf_op jit(solution)/shard_map/all_to_all | solution.py:110
  153.7 5.7 %fusion.7 = f32[1024,256]{1,0:T(8,128)S(1)} fusion(f32[1024,1536]{1,0:T(8,128)} %fusion.16, f32[1024,1536]{1,0:T(8,128)} %copy.33, bf16[1536,1280]{1,0:T(8,128)(2,1)} %all-gather.2.cloned.1.call-done), kind=kOutput, calls=%fused_computation.13 | convolution fusion | flops 808452096 | bytes 14417920 | tf_op jit(solution)/shard_map/dot_general | solution.py:65
  159.4 1.0 slice_bitcast_fusion
  160.4 0.2 convert_reduce_fusion.1
  160.6 0.7 slice_bitcast_fusion.2
  161.3 44.9 %all-to-all-done.1 = bf16[256,4,1024]{2,1,0:T(4,128)(2,1)S(1)} async-done(((bf16[256,4,1024]{2,1,0:T(4,128)(2,1)}), bf16[256,4,1024]{2,1,0:T(4,128)(2,1)S(1)}, u32[]{:S(2)}, u32[]{:S(2)}) %all-to-all-start.1) | async-done | bytes 2097184 | tf_op jit(solution)/shard_map/all_to_all | solution.py:110
  206.2 0.8 convert_reduce_fusion
  207.0 0.6 slice_bitcast_fusion.4
  (12 shorter events, 0.0 us)
Async XLA Ops:
  7.2 82.2 %all-gather.2.cloned.1.call-start = ((), (), s32[]{:S(2)}) async-start(), calls=%async_computation.2 | async-start | bytes 4177920 | tf_op jit(solution)/shard_map/all_gather | solution.py:62
  10.6 3.0 %copy-start.3 = (bf16[1,512,1536]{2,1,0:T(8,128)(2,1)S(1)}, bf16[1,512,1536]{2,1,0:T(8,128)(2,1)}, u32[]{:S(2)}) copy-start(bf16[1,512,1536]{2,1,0:T(8,128)(2,1)} %param.10) | copy-start | bytes 4718596
  14.3 3.0 %copy-start.4 = (bf16[1,512,1536]{2,1,0:T(8,128)(2,1)S(1)}, bf16[1,512,1536]{2,1,0:T(8,128)(2,1)}, u32[]{:S(2)}) copy-start(bf16[1,512,1536]{2,1,0:T(8,128)(2,1)} %param.12) | copy-start | bytes 4718596
  18.1 3.0 %copy-start.7 = (s32[1,12]{1,0:T(1,128)S(1)}, s32[1,12]{1,0:T(1,128)}, u32[]{:S(2)}) copy-start(s32[1,12]{1,0:T(1,128)} %param.13) | copy-start | bytes 148
  27.0 2.2 %copy-start.1 = (bf16[12,1536,128]{2,1,0:T(8,128)(2,1)}, bf16[12,1536,128]{2,1,0:T(8,128)(2,1)S(1)}, u32[]{:S(2)}) copy-start(bf16[12,1536,128]{2,1,0:T(8,128)(2,1)S(1)} %copy.38) | copy-start | bytes 14155780
  41.7 6.7 %copy-start.5 = (bf16[1,512,512]{2,1,0:T(8,128)(2,1)S(1)}, bf16[1,512,512]{2,1,0:T(8,128)(2,1)}, u32[]{:S(2)}) copy-start(bf16[1,512,512]{2,1,0:T(8,128)(2,1)} %param.9) | copy-start | bytes 1572868
  41.7 6.7 %copy-start.6 = (bf16[1,512,512]{2,1,0:T(8,128)(2,1)S(1)}, bf16[1,512,512]{2,1,0:T(8,128)(2,1)}, u32[]{:S(2)}) copy-start(bf16[1,512,512]{2,1,0:T(8,128)(2,1)} %param.8) | copy-start | bytes 1572868
  89.4 4.7 %copy-start = (f32[1024,1536]{1,0:T(8,128)S(1)}, f32[1024,1536]{1,0:T(8,128)}, u32[]{:S(2)}) copy-start(f32[1024,1536]{1,0:T(8,128)} %copy.33) | copy-start | bytes 18874372
  89.4 5.8 %copy-start.2 = (f32[1024,1536]{1,0:T(8,128)S(1)}, f32[1024,1536]{1,0:T(8,128)}, u32[]{:S(2)}) copy-start(f32[1024,1536]{1,0:T(8,128)} %fusion.16) | copy-start | bytes 18874372
  104.6 6.1 %collective-permute-start = (bf16[1024,1024]{1,0:T(8,128)(2,1)}, bf16[1024,1024]{1,0:T(8,128)(2,1)}, u32[]{:S(2)}, u32[]{:S(2)}) collective-permute-start(bf16[1024,1024]{1,0:T(8,128)(2,1)} %pad_maximum_fusion), channel_id=1, source_target_pairs={{0,16},{16,0},{32,48},{48,32},{64,80},{80,64},{96,112},{112,96},{1... | collective-permute-start | bytes 6291464 | tf_op jit(solution)/shard_map/ppermute | solution.py:102
  106.8 37.6 %all-to-all-start = ((bf16[16,16,2560]{2,1,0:T(8,128)(2,1)}), bf16[16,16,2560]{2,1,0:T(8,128)(2,1)S(1)}, u32[]{:S(2)}, u32[]{:S(2)}) async-start(bf16[16,16,2560]{2,1,0:T(8,128)(2,1)} %bitcast.14), calls=%async_computation | async-start | bytes 2621440 | tf_op jit(solution)/shard_map/all_to_all | solution.py:84
  144.4 61.8 %all-to-all-start.1 = ((bf16[256,4,1024]{2,1,0:T(4,128)(2,1)}), bf16[256,4,1024]{2,1,0:T(4,128)(2,1)S(1)}, u32[]{:S(2)}, u32[]{:S(2)}) async-start(bf16[256,4,1024]{2,1,0:T(4,128)(2,1)} %convert_element_type.55), calls=%async_computation.1 | async-start | bytes 4194304 | tf_op jit(solution)/shard_map/all_to_all | solution.py:110
Sparse Core Ops, SparseCore 0:
  10.3 78.9 all-gather.1

commit v5 on v4

--- a/solution.py
+++ b/solution.py
@@ -19,6 +19,29 @@
     return lax.dot_general(
         first_operand, second_operand, (((0,), (0,)), ((), ())), preferred_element_type=jnp.float32
     )
+
+
+def gather_leaf(rows, leaf_count):
+    ring = leaf_count // 2
+    own = lax.axis_index("leaf")
+    upper = own // ring
+    other = lax.ppermute(rows, "leaf", [(i, (i + ring) % leaf_count) for i in range(leaf_count)])
+    pair = jnp.stack([jnp.where(upper == 0, rows, other), jnp.where(upper == 0, other, rows)])
+    ahead = [(i, (i // ring) * ring + (i % ring + 1) % ring) for i in range(leaf_count)]
+    behind = [(i, (i // ring) * ring + (i % ring - 1) % ring) for i in range(leaf_count)]
+    from_behind = []
+    from_ahead = []
+    forward = pair
+    backward = pair
+    for step in range(1, ring // 2 + 1):
+        forward = lax.ppermute(forward, "leaf", ahead)
+        from_behind.append(forward)
+        if step < ring - ring // 2:
+            backward = lax.ppermute(backward, "leaf", behind)
+            from_ahead.append(backward)
+    relative = jnp.stack([pair] + from_ahead + from_behind[::-1])
+    placed = jnp.roll(relative, own % ring, axis=0)
+    return jnp.swapaxes(placed, 0, 1).reshape(leaf_count * rows.shape[0], rows.shape[1])
 
 
 def body(
@@ -59,7 +82,7 @@
     half_work = (0.5 * product + sides).astype(jnp.bfloat16)
     full_work = (product + sides).astype(jnp.bfloat16)
     basis_rows = jnp.concatenate([mid_modes[0], mid_constraint[0]], axis=1)
-    mode_basis = lax.all_gather(basis_rows, "leaf", axis=0, tiled=True)
+    mode_basis = gather_leaf(basis_rows, leaf_count)
     left_sum = jnp.dot(constraint, mode_basis, preferred_element_type=jnp.float32)
     right_sum = jnp.dot(half_work, mode_basis, preferred_element_type=jnp.float32)
     coupling = jnp.dot(full_work, mode_basis[:, :mode_count], preferred_element_type=jnp.float32)

time: 218 us -> 218 us (level)
  starting transfers between devices: 13.2 us -> 28 us
  local copies, waits for them, and re-layouts: 39.1 us -> 53 us
  between operations: 14.2 us -> 0.93 us
  waiting for transfers between devices: 103 us -> 91 us
  matrix products: 34.3 us -> 28.6 us
    all_gather x1 -> x0, waiting for transfers between devices: 36.4 us -> none  [body(): mode_basis = lax.all_gather(basis_rows, 'leaf', axis=0, tiled=True)]
    ppermute x0 -> x8, waiting for transfers between devices: none -> 24.3 us  [the longest x4 15.4 us: gather_leaf(): forward = lax.ppermute(forward, 'leaf', ahead)]
    ppermute x0 -> x8, starting transfers between devices: none -> 14.4 us  [the longest x3 12.8 us: gather_leaf(): backward = lax.ppermute(backward, 'leaf', behind)]
    unnamed x19 -> x38, local copies, waits for them, and re-layouts: 6.47 us -> 14.7 us
    dynamic_slice x0 -> x1, local copies, waits for them, and re-layouts: none -> 2.52 us  [gather_leaf(): placed = jnp.roll(relative, own % ring, axis=0)]
    slice x2, local copies, waits for them, and re-layouts: 0.81 us -> 3.09 us  [body(): constraint = placed[:leaf_order]]
    dot_general x1, matrix products: 4.52 us -> 2.29 us  [body(): jnp.dot(constraint, mode_basis, preferred_element_type=jnp.float32)]
  transfers between devices with their start and end apart: 4 -> 11, of which waited for: 3 -> 7; matrix products, arithmetic and copies ran while one was open for 30% -> 31% of each run, Pallas kernels for 0% -> 0%
where the time goes in v5:
time: 218 us; the launch traced here: 214 us
  waiting for transfers between devices  91 us (42%)
  local copies, waits for them, and re-layouts  53 us (24%)
  matrix products  28.6 us (13%)
  starting transfers between devices  28 us (13%)
  other arithmetic  12.6 us (6%)
    all_to_all x1, waiting for transfers between devices, body(): lax.all_to_all(root_rows.reshape(device_count, root_width // device_count...  44.9 us
    all_to_all x1, waiting for transfers between devices, body(): lax.all_to_all(modal_rows.reshape(leaf_count, mode_count // leaf_count, 2...  21.8 us
    ppermute x4, waiting for transfers between devices, gather_leaf(): forward = lax.ppermute(forward, 'leaf', ahead)  15.4 us
    unnamed x38, local copies, waits for them, and re-layouts  14.7 us
    convert_element_type x2, local copies, waits for them, and re-layouts, body(): sides = placed[leaf_order:].astype(jnp.float32)  13.3 us
    ppermute x3, starting transfers between devices, gather_leaf(): backward = lax.ppermute(backward, 'leaf', behind)  12.8 us
    all_to_all x1, starting transfers between devices, body(): lax.all_to_all(root_rows.reshape(device_count, root_width // device_count...  9.67 us
    concatenate x3, local copies, waits for them, and re-layouts, body(): jnp.concatenate([leaf_modes[0], mass_coupling[0], damp_coupling[0]], axis=0)  9.01 us
  transfers between devices with their start and end apart: 11, of which 7 were waited for; matrix products, arithmetic and copies ran while one was open for 31% of the time, Pallas kernels for 0%

profile of v5, /device:TPU:2, one launch (start us, length us, event | category | flops | bytes accessed | tf_op | source)
XLA Modules:
  0.0 214.1 jit_solution(9475675316619802217)
XLA Ops:
  0.6 1.8 pad_maximum_fusion.9
  2.4 1.6 collective-permute-start
  4.0 1.7 copy.38
  5.7 3.0 %copy.41 = bf16[512,12,128]{2,1,0:T(8,128)(2,1)} copy(bf16[512,12,128]{0,2,1:T(8,128)(2,1)S(1)} %bitcast.95) | data formatting | bytes 3145728 | tf_op jit(solution)/shard_map/concatenate | solution.py:70
  9.4 3.0 %copy.42 = bf16[512,12,128]{2,1,0:T(8,128)(2,1)} copy(bf16[512,12,128]{0,2,1:T(8,128)(2,1)S(1)} %bitcast.96) | data formatting | bytes 3145728 | tf_op jit(solution)/shard_map/concatenate | solution.py:70
  13.2 3.0 %copy.43 = bf16[512,12,128]{2,1,0:T(8,128)(2,1)} copy(bf16[512,12,128]{0,2,1:T(8,128)(2,1)S(1)} %bitcast.97) | data formatting | bytes 3145728 | tf_op jit(solution)/shard_map/concatenate | solution.py:70
  16.2 1.0 select_bitcast_fusion.1
  18.0 5.9 %collective-permute-start.1 = (bf16[2,96,1280]{2,1,0:T(8,128)(2,1)}, bf16[2,96,1280]{2,1,0:T(8,128)(2,1)S(1)}, u32[]{:S(2)}, u32[]{:S(2)}) collective-permute-start(bf16[2,96,1280]{2,1,0:T(8,128)(2,1)} %pad_maximum_fusion.8), channel_id=1, source_target_pairs={{0,7},{1,0},{2,1},{3,2},{4,3},{5,4},{6,5},{7,6},{8,15},{9,8},{10,9... | collective-permute-start | bytes 1474568 | tf_op jit(solution)/shard_map/ppermute | solution.py:40
  23.9 4.6 %fusion = bf16[12,1536,128]{2,0,1:T(8,128)(2,1)S(1)} fusion(bf16[512,12,128]{2,1,0:T(8,128)(2,1)} %copy.43, bf16[512,12,128]{2,1,0:T(8,128)(2,1)} %copy.42, bf16[512,12,128]{2,1,0:T(8,128)(2,1)} %copy.41, s32[12]{0:T(128)S(1)} %bitcast.109), kind=kOutput, calls=%fused_computation.1 | convolution fusion | flops 70779024 | bytes 9437232 | tf_op jit(solution)/shard_map/lbk,bj->ljk/dot_general | solution.py:9
  28.5 1.2 copy.66
  29.8 7.9 %collective-permute-done.4 = bf16[2,96,1280]{2,1,0:T(8,128)(2,1)S(1)} collective-permute-done((bf16[2,96,1280]{2,1,0:T(8,128)(2,1)}, bf16[2,96,1280]{2,1,0:T(8,128)(2,1)S(1)}, u32[]{:S(2)}, u32[]{:S(2)}) %collective-permute-start.4) | collective-permute-done | bytes 491552 | tf_op jit(solution)/shard_map/ppermute | solution.py:37
  37.7 3.2 %slice_convert_fusion = f32[1024,12,128]{2,0,1:T(8,128)} fusion(bf16[1536,12,128]{2,0,1:T(8,128)(2,1)S(1)} %bitcast.92), kind=kLoop, calls=%fused_computation.14 | loop fusion | flops 1572864 | bytes 9437184 | tf_op jit(solution)/shard_map/convert_element_type | solution.py:76
  40.9 1.5 slice.81
  42.5 1.6 copy.45
  44.0 6.6 %copy.46 = f32[1024,12,128]{0,2,1:T(8,128)} copy(f32[1024,12,128]{2,0,1:T(8,128)} %slice_convert_fusion) | data formatting | bytes 12582912 | tf_op jit(solution)/shard_map/convert_element_type | solution.py:76
  50.7 6.7 %copy.47 = f32[1024,1536]{1,0:T(8,128)} copy(f32[1024,1536]{0,1:T(8,128)} %bitcast.91) | data formatting | bytes 12582912 | tf_op jit(solution)/shard_map/convert_element_type | solution.py:76
  57.4 3.2 %collective-permute-start.2 = (bf16[2,96,1280]{2,1,0:T(8,128)(2,1)S(1)}, bf16[2,96,1280]{2,1,0:T(8,128)(2,1)S(1)}, u32[]{:S(2)}, u32[]{:S(2)}) collective-permute-start(bf16[2,96,1280]{2,1,0:T(8,128)(2,1)S(1)} %collective-permute-done.1), channel_id=1, source_target_pairs={{0,7},{1,0},{2,1},{3,2},{4,3},{5,4},{6,5},{7,6},{8,15},{9,8},{10,9... | collective-permute-start | bytes 1474568 | tf_op jit(solution)/shard_map/ppermute | solution.py:40
  60.6 3.0 %fusion.16 = f32[1024,1536]{1,0:T(8,128)S(1)} fusion(bf16[512,1536]{0,1:T(8,128)(2,1)S(1)} %bitcast.101, bf16[512,512]{1,0:T(8,128)(2,1)} %bitcast.107, bf16[512,512]{1,0:T(8,128)(2,1)} %bitcast.108), kind=kOutput, calls=%fused_computation.31 | convolution fusion | flops 1612709888 | bytes 8912896 | tf_op jit(solution)/shard_map/dot_general | solution.py:77
  63.8 1.0 bitcast_dynamic-update-slice_fusion.12
  64.8 4.6 %collective-permute-done.2 = bf16[2,96,1280]{2,1,0:T(8,128)(2,1)S(1)} collective-permute-done((bf16[2,96,1280]{2,1,0:T(8,128)(2,1)S(1)}, bf16[2,96,1280]{2,1,0:T(8,128)(2,1)S(1)}, u32[]{:S(2)}, u32[]{:S(2)}) %collective-permute-start.2) | collective-permute-done | bytes 491552 | tf_op jit(solution)/shard_map/ppermute | solution.py:40
  69.4 3.7 %collective-permute-start.3 = (bf16[2,96,1280]{2,1,0:T(8,128)(2,1)S(1)}, bf16[2,96,1280]{2,1,0:T(8,128)(2,1)S(1)}, u32[]{:S(2)}, u32[]{:S(2)}) collective-permute-start(bf16[2,96,1280]{2,1,0:T(8,128)(2,1)S(1)} %collective-permute-done.2), channel_id=1, source_target_pairs={{0,7},{1,0},{2,1},{3,2},{4,3},{5,4},{6,5},{7,6},{8,15},{9,8},{10,9... | collective-permute-start | bytes 1474568 | tf_op jit(solution)/shard_map/ppermute | solution.py:40
  73.9 2.0 collective-permute-done.6
  75.9 0.8 bitcast_dynamic-update-slice_fusion.8
  76.8 4.2 %collective-permute-done.3 = bf16[2,96,1280]{2,1,0:T(8,128)(2,1)S(1)} collective-permute-done((bf16[2,96,1280]{2,1,0:T(8,128)(2,1)S(1)}, bf16[2,96,1280]{2,1,0:T(8,128)(2,1)S(1)}, u32[]{:S(2)}, u32[]{:S(2)}) %collective-permute-start.3) | collective-permute-done | bytes 491552 | tf_op jit(solution)/shard_map/ppermute | solution.py:40
  81.8 5.5 %collective-permute-done.7 = bf16[2,96,1280]{2,1,0:T(8,128)(2,1)S(1)} collective-permute-done((bf16[2,96,1280]{2,1,0:T(8,128)(2,1)S(1)}, bf16[2,96,1280]{2,1,0:T(8,128)(2,1)S(1)}, u32[]{:S(2)}, u32[]{:S(2)}) %collective-permute-start.7) | collective-permute-done | bytes 491552 | tf_op jit(solution)/shard_map/ppermute | solution.py:37
  87.3 0.8 bitcast_dynamic-update-slice_fusion.4
  89.7 0.8 bitcast_dynamic-update-slice_fusion.14
  93.1 0.8 bitcast_dynamic-update-slice_fusion.7
  93.9 0.9 bitcast_dynamic-update-slice_fusion.5
  94.8 0.8 bitcast_dynamic-update-slice_fusion.3
  95.6 0.8 bitcast_dynamic-update-slice_fusion.1
  96.5 0.9 bitcast_dynamic-update-slice_fusion.15
  97.3 2.5 %constant_dynamic-slice_fusion = bf16[8,2,96,1280]{3,2,0,1:T(8,128)(2,1)S(1)} fusion(bf16[16,2,96,1280]{3,2,0,1:T(8,128)(2,1)} %bitcast_dynamic-update-slice_fusion.15, s32[]{:T(128)S(6)} %select_n.57), kind=kLoop, calls=%fused_computation.71 | loop fusion | bytes 7864324 | tf_op jit(solution)/shard_map/jit(_roll_dynamic)/dynamic_slice | solution.py:43
  99.9 2.3 %convolution_convert_fusion.1 = bf16[512,1280]{1,0:T(8,128)(2,1)S(1)} fusion(bf16[512,1536]{0,1:T(8,128)(2,1)S(1)} %bitcast.102, bf16[1536,1280]{1,0:T(8,128)(2,1)S(1)} %bitcast.98), kind=kOutput, calls=%fused_computation.16 | convolution fusion | flops 2013921280 | bytes 6815744 | tf_op jit(solution)/shard_map/dot_general | solution.py:86
  103.1 4.5 %convolution_convert_fusion = bf16[1024,1280]{1,0:T(8,128)(2,1)S(1)} fusion(bf16[1536,1280]{1,0:T(8,128)(2,1)S(1)} %bitcast.99, f32[1024,1536]{1,0:T(8,128)S(1)} %bitcast.90, f32[1024,1536]{1,0:T(8,128)S(1)} %fusion.16), kind=kOutput, calls=%fused_computation.12 | convolution fusion | flops 4032561152 | bytes 19136512 | tf_op jit(solution)/shard_map/dot_general | solution.py:87
  108.2 1.6 pad_maximum_fusion
  111.4 1.2 pad_maximum_fusion.7
  112.6 3.9 %all-to-all-start = ((bf16[16,16,2560]{2,1,0:T(8,128)(2,1)}), bf16[16,16,2560]{2,1,0:T(8,128)(2,1)S(1)}, u32[]{:S(2)}, u32[]{:S(2)}) async-start(bf16[16,16,2560]{2,1,0:T(8,128)(2,1)} %bitcast.41), calls=%async_computation | async-start | bytes 2621440 | tf_op jit(solution)/shard_map/all_to_all | solution.py:107
  116.5 1.7 fusion.33
  118.2 2.4 %fusion.11 = f32[1024,1024]{1,0:T(8,128)S(1)} fusion(bf16[512,1024]{1,0:T(8,128)(2,1)S(1)} %get-tuple-element.9, bf16[512,1024]{1,0:T(8,128)(2,1)S(1)} %get-tuple-element.6, bf16[512,1024]{1,0:T(8,128)(2,1)S(1)} %slice.92, bf16[512,1024]{1,0:T(8,128)(2,1)S(1)} %get-tuple-element.8), kind=kOutput, calls=%fused_computation.25 | convolution fusion | flops 2155872256 | bytes 8388608 | tf_op jit(solution)/shard_map/dot_general | solution.py:19
  120.6 3.9 %add_convert_fusion.2 = bf16[1024,1024]{1,0:T(8,128)(2,1)} fusion(f32[1024,1024]{1,0:T(8,128)S(1)} %fusion.11, bf16[512,1024]{1,0:T(8,128)(2,1)S(1)} %get-tuple-element.9, bf16[512,1024]{1,0:T(8,128)(2,1)S(1)} %get-tuple-element.6, bf16[512,1024]{1,0:T(8,128)(2,1)S(1)} %slice.92, bf16[512,1024]{1,0:T(8,128)(2,1)S(1)} %get-tuple-element.8), kind=kOutput, calls=%fused_computation.11 | convolution fusion | flops 2157969408 | bytes 10485760 | tf_op jit(solution)/shard_map/dot_general | solution.py:19
  124.6 4.1 %convert_element_type.55 = bf16[256,4,1024]{2,1,0:T(4,128)(2,1)} reshape(bf16[1024,1024]{1,0:T(8,128)(2,1)} %add_convert_fusion.2) | data formatting | bytes 4194304 | tf_op jit(solution)/shard_map/convert_element_type | solution.py:134
  128.7 21.8 %all-to-all-done = bf16[16,16,2560]{2,1,0:T(8,128)(2,1)S(1)} async-done(((bf16[16,16,2560]{2,1,0:T(8,128)(2,1)}), bf16[16,16,2560]{2,1,0:T(8,128)(2,1)S(1)}, u32[]{:S(2)}, u32[]{:S(2)}) %all-to-all-start) | async-done | bytes 1310752 | tf_op jit(solution)/shard_map/all_to_all | solution.py:107
  150.4 9.7 %all-to-all-start.1 = ((bf16[256,4,1024]{2,1,0:T(4,128)(2,1)}), bf16[256,4,1024]{2,1,0:T(4,128)(2,1)S(1)}, u32[]{:S(2)}, u32[]{:S(2)}) async-start(bf16[256,4,1024]{2,1,0:T(4,128)(2,1)} %convert_element_type.55), calls=%async_computation.1 | async-start | bytes 4194304 | tf_op jit(solution)/shard_map/all_to_all | solution.py:133
  160.1 5.7 %fusion.7 = f32[1024,256]{1,0:T(8,128)S(1)} fusion(f32[1024,1536]{1,0:T(8,128)} %copy-done.1, f32[1024,1536]{1,0:T(8,128)} %copy.47, bf16[1536,1280]{1,0:T(8,128)(2,1)} %bitcast.100), kind=kOutput, calls=%fused_computation.13 | convolution fusion | flops 808452096 | bytes 14417920 | tf_op jit(solution)/shard_map/dot_general | solution.py:88
  165.8 1.0 slice_bitcast_fusion
  167.7 44.9 %all-to-all-done.1 = bf16[256,4,1024]{2,1,0:T(4,128)(2,1)S(1)} async-done(((bf16[256,4,1024]{2,1,0:T(4,128)(2,1)}), bf16[256,4,1024]{2,1,0:T(4,128)(2,1)S(1)}, u32[]{:S(2)}, u32[]{:S(2)}) %all-to-all-start.1) | async-done | bytes 2097184 | tf_op jit(solution)/shard_map/all_to_all | solution.py:133
  212.6 0.8 convert_reduce_fusion
  (51 shorter events, 12.7 us)
Async XLA Ops:
  0.6 8.1 %copy-start.3 = (bf16[1,512,1536]{2,1,0:T(8,128)(2,1)S(1)}, bf16[1,512,1536]{2,1,0:T(8,128)(2,1)}, u32[]{:S(2)}) copy-start(bf16[1,512,1536]{2,1,0:T(8,128)(2,1)} %param.10) | copy-start | bytes 4718596
  2.4 13.8 %collective-permute-start = (bf16[96,1280]{1,0:T(8,128)(2,1)}, bf16[96,1280]{1,0:T(8,128)(2,1)}, u32[]{:S(2)}, u32[]{:S(2)}) collective-permute-start(bf16[96,1280]{1,0:T(8,128)(2,1)} %pad_maximum_fusion.9), channel_id=1, source_target_pairs={{0,8},{1,9},{2,10},{3,11},{4,12},{5,13},{6,14},{7,15},{8,0},{9,1},... | collective-permute-start | bytes 737288 | tf_op jit(solution)/shard_map/ppermute | solution.py:28
  9.4 3.0 %copy-start.4 = (bf16[1,512,1536]{2,1,0:T(8,128)(2,1)S(1)}, bf16[1,512,1536]{2,1,0:T(8,128)(2,1)}, u32[]{:S(2)}) copy-start(bf16[1,512,1536]{2,1,0:T(8,128)(2,1)} %param.11) | copy-start | bytes 4718596
  12.4 3.7 %copy-start.6 = (bf16[1,96,1024]{2,1,0:T(8,128)(2,1)S(1)}, bf16[1,96,1024]{2,1,0:T(8,128)(2,1)}, u32[]{:S(2)}) copy-start(bf16[1,96,1024]{2,1,0:T(8,128)(2,1)} %param.15) | copy-start | bytes 589828
  12.4 3.7 %copy-start.7 = (bf16[1,96,256]{2,1,0:T(8,128)(2,1)S(1)}, bf16[1,96,256]{2,1,0:T(8,128)(2,1)}, u32[]{:S(2)}) copy-start(bf16[1,96,256]{2,1,0:T(8,128)(2,1)} %param.14) | copy-start | bytes 147460
  12.4 11.5 %copy-start.8 = (s32[1,12]{1,0:T(1,128)S(1)}, s32[1,12]{1,0:T(1,128)}, u32[]{:S(2)}) copy-start(s32[1,12]{1,0:T(1,128)} %param.13) | copy-start | bytes 148
  18.0 39.4 %collective-permute-start.1 = (bf16[2,96,1280]{2,1,0:T(8,128)(2,1)}, bf16[2,96,1280]{2,1,0:T(8,128)(2,1)S(1)}, u32[]{:S(2)}, u32[]{:S(2)}) collective-permute-start(bf16[2,96,1280]{2,1,0:T(8,128)(2,1)} %pad_maximum_fusion.8), channel_id=1, source_target_pairs={{0,7},{1,0},{2,1},{3,2},{4,3},{5,4},{6,5},{7,6},{8,15},{9,8},{10,9... | collective-permute-start | bytes 1474568 | tf_op jit(solution)/shard_map/ppermute | solution.py:40
  23.9 13.8 %collective-permute-start.4 = (bf16[2,96,1280]{2,1,0:T(8,128)(2,1)}, bf16[2,96,1280]{2,1,0:T(8,128)(2,1)S(1)}, u32[]{:S(2)}, u32[]{:S(2)}) collective-permute-start(bf16[2,96,1280]{2,1,0:T(8,128)(2,1)} %pad_maximum_fusion.8), channel_id=1, source_target_pairs={{0,1},{1,2},{2,3},{3,4},{4,5},{5,6},{6,7},{7,0},{8,9},{9,10},{10,1... | collective-permute-start | bytes 1474568 | tf_op jit(solution)/shard_map/ppermute | solution.py:37
  29.7 8.0 %copy-start = (bf16[12,1536,128]{2,1,0:T(8,128)(2,1)}, bf16[12,1536,128]{2,1,0:T(8,128)(2,1)S(1)}, u32[]{:S(2)}) copy-start(bf16[12,1536,128]{2,1,0:T(8,128)(2,1)S(1)} %copy.66) | copy-start | bytes 14155780
  37.7 26.0 %collective-permute-start.5 = (bf16[2,96,1280]{2,1,0:T(8,128)(2,1)S(1)}, bf16[2,96,1280]{2,1,0:T(8,128)(2,1)S(1)}, u32[]{:S(2)}, u32[]{:S(2)}) collective-permute-start(bf16[2,96,1280]{2,1,0:T(8,128)(2,1)S(1)} %collective-permute-done.4), channel_id=1, source_target_pairs={{0,1},{1,2},{2,3},{3,4},{4,5},{5,6},{6,7},{7,0},{8,9},{9,10},{10,1... | collective-permute-start | bytes 1474568 | tf_op jit(solution)/shard_map/ppermute | solution.py:37
  50.7 10.0 %copy-start.5 = (bf16[512,12,128]{0,2,1:T(8,128)(2,1)S(1)}, bf16[512,12,128]{0,2,1:T(8,128)(2,1)}, u32[]{:S(2)}) copy-start(bf16[512,12,128]{0,2,1:T(8,128)(2,1)} %copy.45) | copy-start | bytes 4718596
  57.4 12.0 %collective-permute-start.2 = (bf16[2,96,1280]{2,1,0:T(8,128)(2,1)S(1)}, bf16[2,96,1280]{2,1,0:T(8,128)(2,1)S(1)}, u32[]{:S(2)}, u32[]{:S(2)}) collective-permute-start(bf16[2,96,1280]{2,1,0:T(8,128)(2,1)S(1)} %collective-permute-done.1), channel_id=1, source_target_pairs={{0,7},{1,0},{2,1},{3,2},{4,3},{5,4},{6,5},{7,6},{8,15},{9,8},{10,9... | collective-permute-start | bytes 1474568 | tf_op jit(solution)/shard_map/ppermute | solution.py:40
  63.7 38.6 %copy-start.1 = (f32[1024,1536]{1,0:T(8,128)}, f32[1024,1536]{1,0:T(8,128)S(1)}, u32[]{:S(2)}) copy-start(f32[1024,1536]{1,0:T(8,128)S(1)} %fusion.16) | copy-start | bytes 18874372
  63.7 12.3 %collective-permute-start.6 = (bf16[2,96,1280]{2,1,0:T(8,128)(2,1)S(1)}, bf16[2,96,1280]{2,1,0:T(8,128)(2,1)S(1)}, u32[]{:S(2)}, u32[]{:S(2)}) collective-permute-start(bf16[2,96,1280]{2,1,0:T(8,128)(2,1)S(1)} %collective-permute-done.5), channel_id=1, source_target_pairs={{0,1},{1,2},{2,3},{3,4},{4,5},{5,6},{6,7},{7,0},{8,9},{9,10},{10,1... | collective-permute-start | bytes 1474568 | tf_op jit(solution)/shard_map/ppermute | solution.py:37
  69.4 11.6 %collective-permute-start.3 = (bf16[2,96,1280]{2,1,0:T(8,128)(2,1)S(1)}, bf16[2,96,1280]{2,1,0:T(8,128)(2,1)S(1)}, u32[]{:S(2)}, u32[]{:S(2)}) collective-permute-start(bf16[2,96,1280]{2,1,0:T(8,128)(2,1)S(1)} %collective-permute-done.2), channel_id=1, source_target_pairs={{0,7},{1,0},{2,1},{3,2},{4,3},{5,4},{6,5},{7,6},{8,15},{9,8},{10,9... | collective-permute-start | bytes 1474568 | tf_op jit(solution)/shard_map/ppermute | solution.py:40
  75.9 11.3 %collective-permute-start.7 = (bf16[2,96,1280]{2,1,0:T(8,128)(2,1)S(1)}, bf16[2,96,1280]{2,1,0:T(8,128)(2,1)S(1)}, u32[]{:S(2)}, u32[]{:S(2)}) collective-permute-start(bf16[2,96,1280]{2,1,0:T(8,128)(2,1)S(1)} %collective-permute-done.6), channel_id=1, source_target_pairs={{0,1},{1,2},{2,3},{3,4},{4,5},{5,6},{6,7},{7,0},{8,9},{9,10},{10,1... | collective-permute-start | bytes 1474568 | tf_op jit(solution)/shard_map/ppermute | solution.py:37
  97.3 5.0 %slice-start = ((s8[6291456]{0:T(1024)(128)(4,1)}), s8[4194304]{0:T(1024)(128)(4,1)S(1)}, s32[]{:S(2)}) async-start(s8[6291456]{0:T(1024)(128)(4,1)} %bitcast.89), calls=%async_computation.2 | async-start | bytes 8388608
  99.8 2.5 %copy-start.2 = (bf16[8,2,96,1280]{3,2,0,1:T(8,128)(2,1)}, bf16[8,2,96,1280]{3,2,0,1:T(8,128)(2,1)S(1)}, u32[]{:S(2)}) copy-start(bf16[8,2,96,1280]{3,2,0,1:T(8,128)(2,1)S(1)} %constant_dynamic-slice_fusion) | copy-start | bytes 11796484
  99.8 3.2 %slice-start.1 = ((s8[6291456]{0:T(1024)(128)(4,1)}), s8[2097152]{0:T(1024)(128)(4,1)S(1)}, s32[]{:S(2)}) async-start(s8[6291456]{0:T(1024)(128)(4,1)} %bitcast.89), calls=%async_computation.3 | async-start | bytes 4194304
  109.8 6.7 %collective-permute-start.8 = (bf16[1024,1024]{1,0:T(8,128)(2,1)}, bf16[1024,1024]{1,0:T(8,128)(2,1)}, u32[]{:S(2)}, u32[]{:S(2)}) collective-permute-start(bf16[1024,1024]{1,0:T(8,128)(2,1)} %pad_maximum_fusion), channel_id=1, source_target_pairs={{0,16},{16,0},{32,48},{48,32},{64,80},{80,64},{96,112},{112,96},{1... | collective-permute-start | bytes 6291464 | tf_op jit(solution)/shard_map/ppermute | solution.py:125
  112.6 37.9 %all-to-all-start = ((bf16[16,16,2560]{2,1,0:T(8,128)(2,1)}), bf16[16,16,2560]{2,1,0:T(8,128)(2,1)S(1)}, u32[]{:S(2)}, u32[]{:S(2)}) async-start(bf16[16,16,2560]{2,1,0:T(8,128)(2,1)} %bitcast.41), calls=%async_computation | async-start | bytes 2621440 | tf_op jit(solution)/shard_map/all_to_all | solution.py:107
  150.4 62.2 %all-to-all-start.1 = ((bf16[256,4,1024]{2,1,0:T(4,128)(2,1)}), bf16[256,4,1024]{2,1,0:T(4,128)(2,1)S(1)}, u32[]{:S(2)}, u32[]{:S(2)}) async-start(bf16[256,4,1024]{2,1,0:T(4,128)(2,1)} %convert_element_type.55), calls=%async_computation.1 | async-start | bytes 4194304 | tf_op jit(solution)/shard_map/all_to_all | solution.py:133

commit v6 on v4

--- a/solution.py
+++ b/solution.py
@@ -80,17 +80,8 @@
         )
         return jnp.concatenate([mass_term, damp_term], axis=1)
 
-    modal_rows = projected_rows(jnp.int32(0), mode_count, 0)
-    modal_recv = lax.all_to_all(
-        modal_rows.reshape(leaf_count, mode_count // leaf_count, 2 * basis_width).astype(jnp.bfloat16),
-        "leaf",
-        0,
-        0,
-        tiled=True,
-    )
-    modal_part = jnp.sum(
-        modal_recv.reshape(leaf_count, mode_count // leaf_count, 2 * basis_width).astype(jnp.float32),
-        axis=0,
+    modal_part = lax.psum_scatter(
+        projected_rows(jnp.int32(0), mode_count, 0), "leaf", scatter_dimension=0, tiled=True
     )
     device_count = group_count * leaf_count
     core_odd = lax.axis_index("group") % 2 == 1

time: 218 us -> 215 us (0.986); the launches traced: 214 us -> 214 us
  waiting for transfers between devices: 103 us -> 108 us
  starting transfers between devices: 13.2 us -> 9.87 us
    reduce_scatter x0 -> x1, waiting for transfers between devices: none -> 71.7 us  [body(): lax.psum_scatter(projected_rows(jnp.int32(0), mode_count, 0), 'leaf', sca...]
    all_to_all x1, waiting for transfers between devices: 44.9 us -> 0.01 us  [body(): lax.all_to_all(root_rows.reshape(device_count, root_width // device_count...]
    all_to_all x1 -> x0, waiting for transfers between devices: 21.6 us -> none  [body(): lax.all_to_all(modal_rows.reshape(leaf_count, mode_count // leaf_count, 2...]
    all_to_all x1 -> x0, starting transfers between devices: 3.87 us -> none  [body(): lax.all_to_all(modal_rows.reshape(leaf_count, mode_count // leaf_count, 2...]
    unnamed x19 -> x21, local copies, waits for them, and re-layouts: 6.47 us -> 7.11 us
  transfers between devices with their start and end apart: 4 -> 4, of which waited for: 3 -> 3; matrix products, arithmetic and copies ran while one was open for 30% -> 29% of each run, Pallas kernels for 0% -> 0%
where the time goes in v6:
time: 215 us; the launch traced here: 214 us
  waiting for transfers between devices  108 us (50%)
  local copies, waits for them, and re-layouts  37.3 us (17%)
  matrix products  33.1 us (15%)
  between operations  14.2 us (7%)
  other arithmetic  12.2 us (6%)
  starting transfers between devices  9.87 us (5%)
    reduce_scatter x1, waiting for transfers between devices, body(): lax.psum_scatter(projected_rows(jnp.int32(0), mode_count, 0), 'leaf', sca...  71.7 us
    all_gather x1, waiting for transfers between devices, body(): mode_basis = lax.all_gather(basis_rows, 'leaf', axis=0, tiled=True)  35.5 us
    convert_element_type x2, local copies, waits for them, and re-layouts, body(): sides = placed[leaf_order:].astype(jnp.float32)  13.3 us
    all_to_all x1, starting transfers between devices, body(): lax.all_to_all(root_rows.reshape(device_count, root_width // device_count...  9.79 us
    concatenate x3, local copies, waits for them, and re-layouts, body(): jnp.concatenate([leaf_modes[0], mass_coupling[0], damp_coupling[0]], axis=0)  9.08 us
    dot_general x6, matrix products, left_product(): lax.dot_general(first_operand, second_operand, (((0,), (0,)), ((), ())),...  7.13 us
    unnamed x21, local copies, waits for them, and re-layouts  7.11 us
    dot_general x1, matrix products, body(): jnp.dot(half_work, mode_basis, preferred_element_type=jnp.float32)  6.61 us
  transfers between devices with their start and end apart: 4, of which 3 were waited for; matrix products, arithmetic and copies ran while one was open for 29% of the time, Pallas kernels for 0%

profile of v6, /device:TPU:2, one launch (start us, length us, event | category | flops | bytes accessed | tf_op | source)
XLA Modules:
  0.0 214.4 jit_solution(18022343488197545717)
XLA Ops:
  7.2 0.0 all-gather.2.cloned.1.call-start
  7.2 1.6 pad_maximum_fusion.8
  8.9 0.0 all-gather.2.cloned.1.call-update
  8.9 0.0 reduce-scatter.2.cloned.1.call-start
  8.9 1.7 copy.26
  10.7 0.0 copy-start.3
  10.7 3.0 %copy.29 = bf16[512,12,128]{2,1,0:T(8,128)(2,1)} copy(bf16[512,12,128]{0,2,1:T(8,128)(2,1)S(1)} %bitcast.40) | data formatting | bytes 3145728 | tf_op jit(solution)/shard_map/concatenate | solution.py:47
  13.7 0.7 copy.25
  14.4 0.0 copy-start.4
  14.4 3.0 %copy.28 = bf16[512,12,128]{2,1,0:T(8,128)(2,1)} copy(bf16[512,12,128]{0,2,1:T(8,128)(2,1)S(1)} %bitcast.41) | data formatting | bytes 3145728 | tf_op jit(solution)/shard_map/concatenate | solution.py:47
  17.5 0.7 copy.24
  18.2 0.0 copy-start.8
  18.2 3.0 %copy.27 = bf16[512,12,128]{2,1,0:T(8,128)(2,1)} copy(bf16[512,12,128]{0,2,1:T(8,128)(2,1)S(1)} %bitcast.42) | data formatting | bytes 3145728 | tf_op jit(solution)/shard_map/concatenate | solution.py:47
  21.2 4.6 %fusion = bf16[12,1536,128]{2,0,1:T(8,128)(2,1)S(1)} fusion(bf16[512,12,128]{2,1,0:T(8,128)(2,1)} %copy.29, bf16[512,12,128]{2,1,0:T(8,128)(2,1)} %copy.28, bf16[512,12,128]{2,1,0:T(8,128)(2,1)} %copy.27, s32[12]{0:T(128)S(1)} %bitcast.49), kind=kOutput, calls=%fused_computation.1 | convolution fusion | flops 70779024 | bytes 9437232 | tf_op jit(solution)/shard_map/lbk,bj->ljk/dot_general | solution.py:9
  25.8 1.2 copy.38
  27.1 2.2 %copy-done.1 = bf16[12,1536,128]{2,1,0:T(8,128)(2,1)} copy-done((bf16[12,1536,128]{2,1,0:T(8,128)(2,1)}, bf16[12,1536,128]{2,1,0:T(8,128)(2,1)S(1)}, u32[]{:S(2)}) %copy-start.1) | copy-done | bytes 4718616
  29.3 0.1 slice.81
  29.4 0.7 copy.31
  30.1 5.1 %slice_convert_fusion = f32[1024,12,128]{2,0,1:T(8,128)} fusion(bf16[1536,12,128]{2,0,1:T(8,128)(2,1)} %bitcast.38), kind=kLoop, calls=%fused_computation.14 | loop fusion | flops 1572864 | bytes 9437184 | tf_op jit(solution)/shard_map/convert_element_type | solution.py:53
  35.3 6.6 %copy.32 = f32[1024,12,128]{0,2,1:T(8,128)} copy(f32[1024,12,128]{2,0,1:T(8,128)} %slice_convert_fusion) | data formatting | bytes 12582912 | tf_op jit(solution)/shard_map/convert_element_type | solution.py:53
  41.9 6.7 %copy.33 = f32[1024,1536]{1,0:T(8,128)} copy(f32[1024,1536]{0,1:T(8,128)} %bitcast.36) | data formatting | bytes 12582912 | tf_op jit(solution)/shard_map/convert_element_type | solution.py:53
  48.6 4.5 %fusion.14 = f32[1024,1536]{1,0:T(8,128)} fusion(bf16[512,1536]{0,1:T(8,128)(2,1)S(1)} %bitcast.43, bf16[512,512]{1,0:T(8,128)(2,1)S(1)} %bitcast.47, bf16[512,512]{1,0:T(8,128)(2,1)S(1)} %bitcast.48), kind=kOutput, calls=%fused_computation.28 | convolution fusion | flops 1612709888 | bytes 8912896 | tf_op jit(solution)/shard_map/dot_general | solution.py:54
  53.0 35.5 %all-gather.2.cloned.1.call-done = bf16[1536,1280]{1,0:T(8,128)(2,1)} async-done(((bf16[96,1280]{1,0:T(8,128)(2,1)}), bf16[1536,1280]{1,0:T(8,128)(2,1)}) %all-gather.2.cloned.1.call-update) | async-done | bytes 3932176 | tf_op jit(solution)/shard_map/all_gather | solution.py:62
  88.6 4.5 %convolution_convert_fusion.1 = bf16[512,1280]{1,0:T(8,128)(2,1)S(1)} fusion(bf16[512,1536]{0,1:T(8,128)(2,1)S(1)} %bitcast.44, bf16[1536,1280]{1,0:T(8,128)(2,1)} %all-gather.2.cloned.1.call-done), kind=kOutput, calls=%fused_computation.16 | convolution fusion | flops 2013921280 | bytes 6815744 | tf_op jit(solution)/shard_map/dot_general | solution.py:63
  93.1 0.1 slice.92
  93.2 1.1 copy-done.2
  94.4 6.6 %convolution_convert_fusion = bf16[1024,1280]{1,0:T(8,128)(2,1)S(1)} fusion(bf16[1536,1280]{1,0:T(8,128)(2,1)} %all-gather.2.cloned.1.call-done, f32[1024,1536]{1,0:T(8,128)S(1)} %copy-done, f32[1024,1536]{1,0:T(8,128)S(1)} %copy-done.2), kind=kOutput, calls=%fused_computation.12 | convolution fusion | flops 4032561152 | bytes 19136512 | tf_op jit(solution)/shard_map/dot_general | solution.py:64
  101.0 1.2 broadcast_select_fusion
  102.1 1.6 pad_maximum_fusion.1
  103.7 0.5 fusion.10
  104.3 0.5 fusion.12
  104.8 0.5 convolution_add_fusion
  105.3 0.5 convolution_add_fusion.1
  105.9 1.8 pad_maximum_fusion
  107.7 0.0 reduce-scatter.2.cloned.1.call-update
  107.7 0.4 collective-permute-done
  108.1 0.2 fusion.31
  108.3 0.6 copy-done.5
  108.9 2.4 %fusion.9 = f32[1024,1024]{1,0:T(8,128)S(1)} fusion(bf16[512,1024]{1,0:T(8,128)(2,1)S(1)} %get-tuple-element.9, bf16[512,1024]{1,0:T(8,128)(2,1)S(1)} %copy-done.5, bf16[512,1024]{1,0:T(8,128)(2,1)S(1)} %slice.92, bf16[512,1024]{1,0:T(8,128)(2,1)S(1)} %get-tuple-element.8), kind=kOutput, calls=%fused_computation.23 | convolution fusion | flops 2155872256 | bytes 8388608 | tf_op jit(solution)/shard_map/dot_general | solution.py:19
  111.3 2.6 %add_convert_fusion.2 = bf16[1024,1024]{1,0:T(8,128)(2,1)S(1)} fusion(f32[1024,1024]{1,0:T(8,128)S(1)} %fusion.9, bf16[512,1024]{1,0:T(8,128)(2,1)S(1)} %get-tuple-element.9, bf16[512,1024]{1,0:T(8,128)(2,1)S(1)} %copy-done.5, bf16[512,1024]{1,0:T(8,128)(2,1)S(1)} %slice.92, bf16[512,1024]{1,0:T(8,128)(2,1)S(1)} %get-tuple-element.8), kind=kOutput, calls=%fused_computation.11 | convolution fusion | flops 2157969408 | bytes 10485760 | tf_op jit(solution)/shard_map/dot_general | solution.py:19
  113.9 2.2 %convert_element_type.46 = bf16[256,4,1024]{2,1,0:T(4,128)(2,1)} reshape(bf16[1024,1024]{1,0:T(8,128)(2,1)S(1)} %add_convert_fusion.2) | data formatting | bytes 4194304 | tf_op jit(solution)/shard_map/convert_element_type | solution.py:102
  116.2 9.8 %all-to-all-start = ((bf16[256,4,1024]{2,1,0:T(4,128)(2,1)}), bf16[256,4,1024]{2,1,0:T(4,128)(2,1)S(1)}, u32[]{:S(2)}, u32[]{:S(2)}) async-start(bf16[256,4,1024]{2,1,0:T(4,128)(2,1)} %convert_element_type.46), calls=%async_computation.1 | async-start | bytes 4194304 | tf_op jit(solution)/shard_map/all_to_all | solution.py:101
  126.0 5.8 %fusion.7 = f32[1024,256]{1,0:T(8,128)S(1)} fusion(f32[1024,1536]{1,0:T(8,128)} %fusion.14, f32[1024,1536]{1,0:T(8,128)} %copy.33, bf16[1536,1280]{1,0:T(8,128)(2,1)} %all-gather.2.cloned.1.call-done), kind=kOutput, calls=%fused_computation.13 | convolution fusion | flops 808452096 | bytes 14417920 | tf_op jit(solution)/shard_map/dot_general | solution.py:65
  131.8 1.0 slice_bitcast_fusion
  132.8 71.7 %reduce-scatter.2.cloned.1.call-done = f32[16,2560]{1,0:T(8,128)} async-done(((f32[256,2560]{1,0:T(8,128)}), f32[16,2560]{1,0:T(8,128)}) %reduce-scatter.2.cloned.1.call-update) | async-done | bytes 163856 | tf_op jit(solution)/shard_map/reduce_scatter | solution.py:83
  204.5 1.6 slice_bitcast_fusion.2
  206.1 0.8 convert_reduce_fusion
  206.9 0.6 slice_bitcast_fusion.4
  (14 shorter events, 0.0 us)
Async XLA Ops:
  7.2 81.4 %all-gather.2.cloned.1.call-start = ((), (), s32[]{:S(2)}) async-start(), calls=%async_computation.2 | async-start | bytes 4177920 | tf_op jit(solution)/shard_map/all_gather | solution.py:62
  8.9 195.6 %reduce-scatter.2.cloned.1.call-start = ((), (), s32[]{:S(2)}) async-start(), calls=%async_computation.3 | async-start | bytes 2785280 | tf_op jit(solution)/shard_map/reduce_scatter | solution.py:83
  10.7 3.0 %copy-start.3 = (bf16[1,512,1536]{2,1,0:T(8,128)(2,1)S(1)}, bf16[1,512,1536]{2,1,0:T(8,128)(2,1)}, u32[]{:S(2)}) copy-start(bf16[1,512,1536]{2,1,0:T(8,128)(2,1)} %param.10) | copy-start | bytes 4718596
  14.4 3.0 %copy-start.4 = (bf16[1,512,1536]{2,1,0:T(8,128)(2,1)S(1)}, bf16[1,512,1536]{2,1,0:T(8,128)(2,1)}, u32[]{:S(2)}) copy-start(bf16[1,512,1536]{2,1,0:T(8,128)(2,1)} %param.12) | copy-start | bytes 4718596
  18.2 3.0 %copy-start.8 = (s32[1,12]{1,0:T(1,128)S(1)}, s32[1,12]{1,0:T(1,128)}, u32[]{:S(2)}) copy-start(s32[1,12]{1,0:T(1,128)} %param.13) | copy-start | bytes 148
  27.1 2.2 %copy-start.1 = (bf16[12,1536,128]{2,1,0:T(8,128)(2,1)}, bf16[12,1536,128]{2,1,0:T(8,128)(2,1)S(1)}, u32[]{:S(2)}) copy-start(bf16[12,1536,128]{2,1,0:T(8,128)(2,1)S(1)} %copy.38) | copy-start | bytes 14155780
  41.9 6.7 %copy-start.6 = (bf16[1,512,512]{2,1,0:T(8,128)(2,1)S(1)}, bf16[1,512,512]{2,1,0:T(8,128)(2,1)}, u32[]{:S(2)}) copy-start(bf16[1,512,512]{2,1,0:T(8,128)(2,1)} %param.9) | copy-start | bytes 1572868
  41.9 6.7 %copy-start.7 = (bf16[1,512,512]{2,1,0:T(8,128)(2,1)S(1)}, bf16[1,512,512]{2,1,0:T(8,128)(2,1)}, u32[]{:S(2)}) copy-start(bf16[1,512,512]{2,1,0:T(8,128)(2,1)} %param.8) | copy-start | bytes 1572868
  88.6 4.7 %copy-start = (f32[1024,1536]{1,0:T(8,128)S(1)}, f32[1024,1536]{1,0:T(8,128)}, u32[]{:S(2)}) copy-start(f32[1024,1536]{1,0:T(8,128)} %copy.33) | copy-start | bytes 18874372
  88.6 5.8 %copy-start.2 = (f32[1024,1536]{1,0:T(8,128)S(1)}, f32[1024,1536]{1,0:T(8,128)}, u32[]{:S(2)}) copy-start(f32[1024,1536]{1,0:T(8,128)} %fusion.14) | copy-start | bytes 18874372
  103.7 4.4 %collective-permute-start = (bf16[1024,1024]{1,0:T(8,128)(2,1)}, bf16[1024,1024]{1,0:T(8,128)(2,1)S(1)}, u32[]{:S(2)}, u32[]{:S(2)}) collective-permute-start(bf16[1024,1024]{1,0:T(8,128)(2,1)} %pad_maximum_fusion.1), channel_id=1, source_target_pairs={{0,16},{16,0},{32,48},{48,32},{64,80},{80,64},{96,112},{112,96},{1... | collective-permute-start | bytes 6291464 | tf_op jit(solution)/shard_map/ppermute | solution.py:93
  107.7 1.2 copy-start.5
  116.2 89.9 %all-to-all-start = ((bf16[256,4,1024]{2,1,0:T(4,128)(2,1)}), bf16[256,4,1024]{2,1,0:T(4,128)(2,1)S(1)}, u32[]{:S(2)}, u32[]{:S(2)}) async-start(bf16[256,4,1024]{2,1,0:T(4,128)(2,1)} %convert_element_type.46), calls=%async_computation.1 | async-start | bytes 4194304 | tf_op jit(solution)/shard_map/all_to_all | solution.py:101
Sparse Core Ops, SparseCore 0:
  10.3 78.1 all-gather.1
  107.8 96.6 reduce-scatter.1

commit v7 on v5

--- a/solution.py
+++ b/solution.py
@@ -82,7 +82,14 @@
     half_work = (0.5 * product + sides).astype(jnp.bfloat16)
     full_work = (product + sides).astype(jnp.bfloat16)
     basis_rows = jnp.concatenate([mid_modes[0], mid_constraint[0]], axis=1)
-    mode_basis = gather_leaf(basis_rows, leaf_count)
+    split_at = basis_width // 2
+    mode_basis = jnp.concatenate(
+        [
+            lax.all_gather(basis_rows[:, :split_at], "leaf", axis=0, tiled=True),
+            gather_leaf(basis_rows[:, split_at:], leaf_count),
+        ],
+        axis=1,
+    )
     left_sum = jnp.dot(constraint, mode_basis, preferred_element_type=jnp.float32)
     right_sum = jnp.dot(half_work, mode_basis, preferred_element_type=jnp.float32)
     coupling = jnp.dot(full_work, mode_basis[:, :mode_count], preferred_element_type=jnp.float32)
@@ -103,17 +110,8 @@
         )
         return jnp.concatenate([mass_term, damp_term], axis=1)
 
-    modal_rows = projected_rows(jnp.int32(0), mode_count, 0)
-    modal_recv = lax.all_to_all(
-        modal_rows.reshape(leaf_count, mode_count // leaf_count, 2 * basis_width).astype(jnp.bfloat16),
-        "leaf",
-        0,
-        0,
-        tiled=True,
-    )
-    modal_part = jnp.sum(
-        modal_recv.reshape(leaf_count, mode_count // leaf_count, 2 * basis_width).astype(jnp.float32),
-        axis=0,
+    modal_part = lax.psum_scatter(
+        projected_rows(jnp.int32(0), mode_count, 0), "leaf", scatter_dimension=0, tiled=True
     )
     device_count = group_count * leaf_count
     core_odd = lax.axis_index("group") % 2 == 1

time: 218 us -> 266 us (1.22); the launches traced: 214 us -> 265 us
  waiting for transfers between devices: 91 us -> 136 us
  between operations: 0.93 us -> 14.5 us
  local copies, waits for them, and re-layouts: 53 us -> 42.5 us
  matrix products: 28.6 us -> 36.7 us
  starting transfers between devices: 28 us -> 24 us
    reduce_scatter x0 -> x1, waiting for transfers between devices: none -> 71.6 us  [body(): lax.psum_scatter(projected_rows(jnp.int32(0), mode_count, 0), 'leaf', sca...]
    all_gather x0 -> x1, waiting for transfers between devices: none -> 51.5 us  [body(): lax.all_gather(basis_rows[:, :split_at], 'leaf', axis=0, tiled=True)]
    all_to_all x1, waiting for transfers between devices: 44.9 us -> 0.01 us  [body(): lax.all_to_all(root_rows.reshape(device_count, root_width // device_count...]
    all_to_all x1 -> x0, waiting for transfers between devices: 21.8 us -> none  [body(): lax.all_to_all(modal_rows.reshape(leaf_count, mode_count // leaf_count, 2...]
    ppermute x3, waiting for transfers between devices: 8.89 us -> 0.01 us  [gather_leaf(): backward = lax.ppermute(backward, 'leaf', behind)]
    unnamed x38 -> x44, local copies, waits for them, and re-layouts: 14.7 us -> 6.38 us
    all_to_all x1 -> x0, starting transfers between devices: 3.92 us -> none  [body(): lax.all_to_all(modal_rows.reshape(leaf_count, mode_count // leaf_count, 2...]
    dot_general x1, local copies, waits for them, and re-layouts: 1.21 us -> 4 us  [to_middle(): jnp.einsum('lbk,bj->ljk', stacked.reshape(rows_total, block_count, block_...]
  transfers between devices with their start and end apart: 11 -> 12, of which waited for: 7 -> 5; matrix products, arithmetic and copies ran while one was open for 31% -> 26% of each run, Pallas kernels for 0% -> 0%
where the time goes in v7:
time: 266 us; the launch traced here: 265 us
  waiting for transfers between devices  136 us (51%)
  local copies, waits for them, and re-layouts  42.5 us (16%)
  matrix products  36.7 us (14%)
  starting transfers between devices  24 us (9%)
  between operations  14.5 us (5%)
  other arithmetic  11.3 us (4%)
    reduce_scatter x1, waiting for transfers between devices, body(): lax.psum_scatter(projected_rows(jnp.int32(0), mode_count, 0), 'leaf', sca...  71.6 us
    all_gather x1, waiting for transfers between devices, body(): lax.all_gather(basis_rows[:, :split_at], 'leaf', axis=0, tiled=True)  51.5 us
    convert_element_type x2, local copies, waits for them, and re-layouts, body(): sides = placed[leaf_order:].astype(jnp.float32)  13.2 us
    ppermute x3, starting transfers between devices, gather_leaf(): backward = lax.ppermute(backward, 'leaf', behind)  12.8 us
    ppermute x4, waiting for transfers between devices, gather_leaf(): forward = lax.ppermute(forward, 'leaf', ahead)  12.7 us
    all_to_all x1, starting transfers between devices, body(): lax.all_to_all(root_rows.reshape(device_count, root_width // device_count...  9.5 us
    concatenate x3, local copies, waits for them, and re-layouts, body(): jnp.concatenate([leaf_modes[0], mass_coupling[0], damp_coupling[0]], axis=0)  9.17 us
    dot_general x1, matrix products, to_middle(): jnp.einsum('lbk,bj->ljk', stacked.reshape(rows_total, block_count, block_...  7.27 us
  transfers between devices with their start and end apart: 12, of which 5 were waited for; matrix products, arithmetic and copies ran while one was open for 26% of the time, Pallas kernels for 0%

profile of v7, /device:TPU:2, one launch (start us, length us, event | category | flops | bytes accessed | tf_op | source)
XLA Modules:
  0.0 265.4 jit_solution(1018713624280620851)
XLA Ops:
  7.2 1.6 slice.94
  8.8 1.6 collective-permute-start
  10.4 1.7 copy.26
  12.1 3.1 %copy.29 = bf16[512,12,128]{2,1,0:T(8,128)(2,1)} copy(bf16[512,12,128]{0,2,1:T(8,128)(2,1)S(1)} %bitcast.71) | data formatting | bytes 3145728 | tf_op jit(solution)/shard_map/concatenate | solution.py:70
  15.1 0.7 copy.27
  15.9 3.1 %copy.30 = bf16[512,12,128]{2,1,0:T(8,128)(2,1)} copy(bf16[512,12,128]{0,2,1:T(8,128)(2,1)S(1)} %bitcast.72) | data formatting | bytes 3145728 | tf_op jit(solution)/shard_map/concatenate | solution.py:70
  18.9 0.7 copy.25
  19.6 3.0 %copy.28 = bf16[512,12,128]{2,1,0:T(8,128)(2,1)} copy(bf16[512,12,128]{0,2,1:T(8,128)(2,1)S(1)} %bitcast.73) | data formatting | bytes 3145728 | tf_op jit(solution)/shard_map/concatenate | solution.py:70
  22.7 7.3 %fusion = bf16[12,1536,128]{2,0,1:T(8,128)(2,1)} fusion(bf16[512,12,128]{2,1,0:T(8,128)(2,1)} %copy.30, bf16[512,12,128]{2,1,0:T(8,128)(2,1)} %copy.29, bf16[512,12,128]{2,1,0:T(8,128)(2,1)} %copy.28, s32[12]{0:T(128)S(1)} %bitcast.83), kind=kOutput, calls=%fused_computation.1 | convolution fusion | flops 70779024 | bytes 9437232 | tf_op jit(solution)/shard_map/lbk,bj->ljk/dot_general | solution.py:9
  30.0 4.0 %copy.40 = bf16[12,1536,128]{2,1,0:T(8,128)(2,1)S(1)} copy(bf16[12,1536,128]{2,0,1:T(8,128)(2,1)} %fusion) | data formatting | bytes 9437184 | tf_op jit(solution)/shard_map/lbk,bj->ljk/dot_general | solution.py:9
  34.0 2.1 copy-done
  36.2 0.7 copy.32
  37.0 0.8 select_bitcast_fusion.1
  37.9 5.9 %collective-permute-start.1 = (bf16[2,96,640]{2,1,0:T(8,128)(2,1)S(1)}, bf16[2,96,640]{2,1,0:T(8,128)(2,1)S(1)}, u32[]{:S(2)}, u32[]{:S(2)}) collective-permute-start(bf16[2,96,640]{2,1,0:T(8,128)(2,1)S(1)} %pad_maximum_fusion.11), channel_id=1, source_target_pairs={{0,7},{1,0},{2,1},{3,2},{4,3},{5,4},{6,5},{7,6},{8,15},{9,8},{10,9... | collective-permute-start | bytes 737288 | tf_op jit(solution)/shard_map/ppermute | solution.py:40
  43.8 5.1 %slice_convert_fusion = f32[1024,12,128]{2,0,1:T(8,128)} fusion(bf16[1536,12,128]{2,0,1:T(8,128)(2,1)} %bitcast.69), kind=kLoop, calls=%fused_computation.15 | loop fusion | flops 1572864 | bytes 9437184 | tf_op jit(solution)/shard_map/convert_element_type | solution.py:76
  48.9 3.5 %collective-permute-start.2 = (bf16[2,96,640]{2,1,0:T(8,128)(2,1)S(1)}, bf16[2,96,640]{2,1,0:T(8,128)(2,1)S(1)}, u32[]{:S(2)}, u32[]{:S(2)}) collective-permute-start(bf16[2,96,640]{2,1,0:T(8,128)(2,1)S(1)} %collective-permute-done.1), channel_id=1, source_target_pairs={{0,7},{1,0},{2,1},{3,2},{4,3},{5,4},{6,5},{7,6},{8,15},{9,8},{10,9... | collective-permute-start | bytes 737288 | tf_op jit(solution)/shard_map/ppermute | solution.py:40
  52.5 4.5 %fusion.14 = f32[1024,1536]{1,0:T(8,128)} fusion(bf16[512,1536]{0,1:T(8,128)(2,1)S(1)} %bitcast.76, bf16[512,512]{1,0:T(8,128)(2,1)S(1)} %bitcast.81, bf16[512,512]{1,0:T(8,128)(2,1)S(1)} %bitcast.82), kind=kOutput, calls=%fused_computation.30 | convolution fusion | flops 1612709888 | bytes 8912896 | tf_op jit(solution)/shard_map/dot_general | solution.py:77
  57.0 6.6 %copy.33 = f32[1024,12,128]{0,2,1:T(8,128)} copy(f32[1024,12,128]{2,0,1:T(8,128)} %slice_convert_fusion) | data formatting | bytes 12582912 | tf_op jit(solution)/shard_map/convert_element_type | solution.py:76
  63.5 6.6 %copy.34 = f32[1024,1536]{1,0:T(8,128)} copy(f32[1024,1536]{0,1:T(8,128)} %bitcast.67) | data formatting | bytes 12582912 | tf_op jit(solution)/shard_map/convert_element_type | solution.py:76
  70.3 3.3 %collective-permute-start.3 = (bf16[2,96,640]{2,1,0:T(8,128)(2,1)S(1)}, bf16[2,96,640]{2,1,0:T(8,128)(2,1)S(1)}, u32[]{:S(2)}, u32[]{:S(2)}) collective-permute-start(bf16[2,96,640]{2,1,0:T(8,128)(2,1)S(1)} %collective-permute-done.2), channel_id=1, source_target_pairs={{0,7},{1,0},{2,1},{3,2},{4,3},{5,4},{6,5},{7,6},{8,15},{9,8},{10,9... | collective-permute-start | bytes 737288 | tf_op jit(solution)/shard_map/ppermute | solution.py:40
  73.7 4.1 %collective-permute-done.6 = bf16[2,96,640]{2,1,0:T(8,128)(2,1)S(1)} collective-permute-done((bf16[2,96,640]{2,1,0:T(8,128)(2,1)S(1)}, bf16[2,96,640]{2,1,0:T(8,128)(2,1)S(1)}, u32[]{:S(2)}, u32[]{:S(2)}) %collective-permute-start.6) | collective-permute-done | bytes 245792 | tf_op jit(solution)/shard_map/ppermute | solution.py:37
  77.9 8.6 %collective-permute-done.7 = bf16[2,96,640]{2,1,0:T(8,128)(2,1)S(1)} collective-permute-done((bf16[2,96,640]{2,1,0:T(8,128)(2,1)S(1)}, bf16[2,96,640]{2,1,0:T(8,128)(2,1)S(1)}, u32[]{:S(2)}, u32[]{:S(2)}) %collective-permute-start.7) | collective-permute-done | bytes 245792 | tf_op jit(solution)/shard_map/ppermute | solution.py:37
  87.0 0.2 dynamic-slice_bitcast_fusion
  87.2 1.4 copy.35
  88.6 51.5 %all-gather.2.cloned.1.call-done = bf16[1536,640]{1,0:T(8,128)(2,1)} async-done(((bf16[96,640]{1,0:T(8,128)(2,1)}), bf16[1536,640]{1,0:T(8,128)(2,1)}) %all-gather.2.cloned.1.call-update) | async-done | bytes 1966096 | tf_op jit(solution)/shard_map/all_gather | solution.py:88
  140.1 5.0 %convolution_convert_fusion.1 = bf16[512,1280]{1,0:T(8,128)(2,1)S(1)} fusion(bf16[512,1536]{0,1:T(8,128)(2,1)} %bitcast.77, bf16[1536,640]{1,0:T(8,128)(2,1)} %bitcast.74, bf16[1536,640]{1,0:T(8,128)(2,1)} %all-gather.2.cloned.1.call-done), kind=kOutput, calls=%fused_computation.17 | convolution fusion | flops 2021785600 | bytes 6815744 | tf_op jit(solution)/shard_map/dot_general | solution.py:93
  145.1 0.1 slice.101
  145.3 7.1 %convolution_convert_fusion = bf16[1024,1280]{1,0:T(8,128)(2,1)S(1)} fusion(f32[1024,1536]{1,0:T(8,128)S(1)} %bitcast.66, f32[1024,1536]{1,0:T(8,128)} %fusion.14, bf16[1536,640]{1,0:T(8,128)(2,1)S(1)} %bitcast.75, bf16[1536,640]{1,0:T(8,128)(2,1)S(1)} %copy-done.7), kind=kOutput, calls=%fused_computation.13 | convolution fusion | flops 4040425472 | bytes 19136512 | tf_op jit(solution)/shard_map/dot_general | solution.py:94
  152.4 1.1 broadcast_select_fusion
  153.5 1.6 pad_maximum_fusion.4
  155.1 0.5 fusion.10
  155.6 0.5 fusion.12
  156.1 0.5 convolution_add_fusion
  156.7 0.5 convolution_add_fusion.1
  157.2 1.8 pad_maximum_fusion.1
  159.0 0.4 collective-permute-done.8
  159.5 0.2 fusion.33
  159.6 0.6 copy-done.5
  160.2 2.4 fusion.9
  162.6 2.6 add_convert_fusion.2
  165.3 2.2 convert_element_type.46
  167.5 9.5 %all-to-all-start = ((bf16[256,4,1024]{2,1,0:T(4,128)(2,1)}), bf16[256,4,1024]{2,1,0:T(4,128)(2,1)S(1)}, u32[]{:S(2)}, u32[]{:S(2)}) async-start(bf16[256,4,1024]{2,1,0:T(4,128)(2,1)} %convert_element_type.46), calls=%async_computation.1 | async-start | bytes 4194304 | tf_op jit(solution)/shard_map/all_to_all | solution.py:131
  177.0 5.8 %fusion.7 = f32[1024,256]{1,0:T(8,128)S(1)} fusion(f32[1024,1536]{1,0:T(8,128)} %fusion.14, f32[1024,1536]{1,0:T(8,128)} %copy.34, bf16[1536,640]{1,0:T(8,128)(2,1)} %all-gather.2.cloned.1.call-done), kind=kOutput, calls=%fused_computation.14 | convolution fusion | flops 808452096 | bytes 14417920 | tf_op jit(solution)/shard_map/dot_general | solution.py:95
  182.8 1.0 slice_bitcast_fusion
  183.8 71.6 %reduce-scatter.2.cloned.1.call-done = f32[16,2560]{1,0:T(8,128)} async-done(((f32[256,2560]{1,0:T(8,128)}), f32[16,2560]{1,0:T(8,128)}) %reduce-scatter.2.cloned.1.call-update) | async-done | bytes 163856 | tf_op jit(solution)/shard_map/reduce_scatter | solution.py:113
  255.5 1.6 slice_bitcast_fusion.2
  257.1 0.8 convert_reduce_fusion
  257.9 0.6 slice_bitcast_fusion.4
  (61 shorter events, 1.0 us)
Async XLA Ops:
  7.2 132.9 %all-gather.2.cloned.1.call-start = ((), (), s32[]{:S(2)}) async-start(), calls=%async_computation.2 | async-start | bytes 2088960 | tf_op jit(solution)/shard_map/all_gather | solution.py:88
  8.8 6.4 %copy-start.2 = (bf16[1,512,1536]{2,1,0:T(8,128)(2,1)S(1)}, bf16[1,512,1536]{2,1,0:T(8,128)(2,1)}, u32[]{:S(2)}) copy-start(bf16[1,512,1536]{2,1,0:T(8,128)(2,1)} %param.11) | copy-start | bytes 4718596
  8.8 28.2 %collective-permute-start = (bf16[96,640]{1,0:T(8,128)(2,1)}, bf16[96,640]{1,0:T(8,128)(2,1)S(1)}, u32[]{:S(2)}, u32[]{:S(2)}) collective-permute-start(bf16[96,640]{1,0:T(8,128)(2,1)} %slice.94), channel_id=1, source_target_pairs={{0,8},{1,9},{2,10},{3,11},{4,12},{5,13},{6,14},{7,15},{8,0},{9,1},... | collective-permute-start | bytes 368648 | tf_op jit(solution)/shard_map/ppermute | solution.py:28
  15.9 3.1 %copy-start.3 = (bf16[1,512,1536]{2,1,0:T(8,128)(2,1)S(1)}, bf16[1,512,1536]{2,1,0:T(8,128)(2,1)}, u32[]{:S(2)}) copy-start(bf16[1,512,1536]{2,1,0:T(8,128)(2,1)} %param.12) | copy-start | bytes 4718596
  18.9 3.7 %copy-start.11 = (s32[1,12]{1,0:T(1,128)S(1)}, s32[1,12]{1,0:T(1,128)}, u32[]{:S(2)}) copy-start(s32[1,12]{1,0:T(1,128)} %param.13) | copy-start | bytes 148
  34.0 2.1 copy-start
  36.1 0.9 copy-start.6
  36.1 0.9 copy-start.8
  36.9 15.6 %copy-start.4 = (bf16[512,12,128]{0,2,1:T(8,128)(2,1)}, bf16[512,12,128]{0,2,1:T(8,128)(2,1)S(1)}, u32[]{:S(2)}) copy-start(bf16[512,12,128]{0,2,1:T(8,128)(2,1)S(1)} %copy.32) | copy-start | bytes 4718596
  37.9 14.6 %copy-start.9 = (bf16[1,512,512]{2,1,0:T(8,128)(2,1)S(1)}, bf16[1,512,512]{2,1,0:T(8,128)(2,1)}, u32[]{:S(2)}) copy-start(bf16[1,512,512]{2,1,0:T(8,128)(2,1)} %param.9) | copy-start | bytes 1572868
  37.9 14.6 %copy-start.10 = (bf16[1,512,512]{2,1,0:T(8,128)(2,1)S(1)}, bf16[1,512,512]{2,1,0:T(8,128)(2,1)}, u32[]{:S(2)}) copy-start(bf16[1,512,512]{2,1,0:T(8,128)(2,1)} %param.8) | copy-start | bytes 1572868
  37.9 11.0 %collective-permute-start.1 = (bf16[2,96,640]{2,1,0:T(8,128)(2,1)S(1)}, bf16[2,96,640]{2,1,0:T(8,128)(2,1)S(1)}, u32[]{:S(2)}, u32[]{:S(2)}) collective-permute-start(bf16[2,96,640]{2,1,0:T(8,128)(2,1)S(1)} %pad_maximum_fusion.11), channel_id=1, source_target_pairs={{0,7},{1,0},{2,1},{3,2},{4,3},{5,4},{6,5},{7,6},{8,15},{9,8},{10,9... | collective-permute-start | bytes 737288 | tf_op jit(solution)/shard_map/ppermute | solution.py:40
  43.8 8.6 %collective-permute-start.4 = (bf16[2,96,640]{2,1,0:T(8,128)(2,1)S(1)}, bf16[2,96,640]{2,1,0:T(8,128)(2,1)S(1)}, u32[]{:S(2)}, u32[]{:S(2)}) collective-permute-start(bf16[2,96,640]{2,1,0:T(8,128)(2,1)S(1)} %pad_maximum_fusion.11), channel_id=1, source_target_pairs={{0,1},{1,2},{2,3},{3,4},{4,5},{5,6},{6,7},{7,0},{8,9},{9,10},{10,1... | collective-permute-start | bytes 737288 | tf_op jit(solution)/shard_map/ppermute | solution.py:37
  48.9 21.4 %collective-permute-start.2 = (bf16[2,96,640]{2,1,0:T(8,128)(2,1)S(1)}, bf16[2,96,640]{2,1,0:T(8,128)(2,1)S(1)}, u32[]{:S(2)}, u32[]{:S(2)}) collective-permute-start(bf16[2,96,640]{2,1,0:T(8,128)(2,1)S(1)} %collective-permute-done.1), channel_id=1, source_target_pairs={{0,7},{1,0},{2,1},{3,2},{4,3},{5,4},{6,5},{7,6},{8,15},{9,8},{10,9... | collective-permute-start | bytes 737288 | tf_op jit(solution)/shard_map/ppermute | solution.py:40
  52.5 17.7 %collective-permute-start.5 = (bf16[2,96,640]{2,1,0:T(8,128)(2,1)S(1)}, bf16[2,96,640]{2,1,0:T(8,128)(2,1)S(1)}, u32[]{:S(2)}, u32[]{:S(2)}) collective-permute-start(bf16[2,96,640]{2,1,0:T(8,128)(2,1)S(1)} %collective-permute-done.4), channel_id=1, source_target_pairs={{0,1},{1,2},{2,3},{3,4},{4,5},{5,6},{6,7},{7,0},{8,9},{9,10},{10,1... | collective-permute-start | bytes 737288 | tf_op jit(solution)/shard_map/ppermute | solution.py:37
  70.1 185.3 %reduce-scatter.2.cloned.1.call-start = ((), (), s32[]{:S(2)}) async-start(), calls=%async_computation.3 | async-start | bytes 2785280 | tf_op jit(solution)/shard_map/reduce_scatter | solution.py:113
  70.2 7.6 %collective-permute-start.6 = (bf16[2,96,640]{2,1,0:T(8,128)(2,1)S(1)}, bf16[2,96,640]{2,1,0:T(8,128)(2,1)S(1)}, u32[]{:S(2)}, u32[]{:S(2)}) collective-permute-start(bf16[2,96,640]{2,1,0:T(8,128)(2,1)S(1)} %collective-permute-done.5), channel_id=1, source_target_pairs={{0,1},{1,2},{2,3},{3,4},{4,5},{5,6},{6,7},{7,0},{8,9},{9,10},{10,1... | collective-permute-start | bytes 737288 | tf_op jit(solution)/shard_map/ppermute | solution.py:37
  70.3 7.5 %collective-permute-start.3 = (bf16[2,96,640]{2,1,0:T(8,128)(2,1)S(1)}, bf16[2,96,640]{2,1,0:T(8,128)(2,1)S(1)}, u32[]{:S(2)}, u32[]{:S(2)}) collective-permute-start(bf16[2,96,640]{2,1,0:T(8,128)(2,1)S(1)} %collective-permute-done.2), channel_id=1, source_target_pairs={{0,7},{1,0},{2,1},{3,2},{4,3},{5,4},{6,5},{7,6},{8,15},{9,8},{10,9... | collective-permute-start | bytes 737288 | tf_op jit(solution)/shard_map/ppermute | solution.py:40
  77.8 8.7 %collective-permute-start.7 = (bf16[2,96,640]{2,1,0:T(8,128)(2,1)S(1)}, bf16[2,96,640]{2,1,0:T(8,128)(2,1)S(1)}, u32[]{:S(2)}, u32[]{:S(2)}) collective-permute-start(bf16[2,96,640]{2,1,0:T(8,128)(2,1)S(1)} %collective-permute-done.6), channel_id=1, source_target_pairs={{0,1},{1,2},{2,3},{3,4},{4,5},{5,6},{6,7},{7,0},{8,9},{9,10},{10,1... | collective-permute-start | bytes 737288 | tf_op jit(solution)/shard_map/ppermute | solution.py:37
  87.2 58.1 %slice-start = ((s8[6291456]{0:T(1024)(128)(4,1)}), s8[2097152]{0:T(1024)(128)(4,1)S(1)}, s32[]{:S(2)}) async-start(s8[6291456]{0:T(1024)(128)(4,1)} %bitcast.65), calls=%async_computation.4 | async-start | bytes 4194304
  140.1 5.2 %slice-start.1 = ((s8[6291456]{0:T(1024)(128)(4,1)}), s8[4194304]{0:T(1024)(128)(4,1)S(1)}, s32[]{:S(2)}) async-start(s8[6291456]{0:T(1024)(128)(4,1)} %bitcast.65), calls=%async_computation.5 | async-start | bytes 8388608
  140.1 5.2 %copy-start.1 = (bf16[2,8,96,640]{3,2,1,0:T(8,128)(2,1)S(1)}, bf16[2,8,96,640]{3,2,1,0:T(8,128)(2,1)}, u32[]{:S(2)}) copy-start(bf16[2,8,96,640]{3,2,1,0:T(8,128)(2,1)} %copy.35) | copy-start | bytes 5898244
  140.1 5.2 %copy-start.7 = (bf16[1536,640]{1,0:T(8,128)(2,1)S(1)}, bf16[1536,640]{1,0:T(8,128)(2,1)}, u32[]{:S(2)}) copy-start(bf16[1536,640]{1,0:T(8,128)(2,1)} %all-gather.2.cloned.1.call-done) | copy-start | bytes 5898244
  155.1 4.4 %collective-permute-start.8 = (bf16[1024,1024]{1,0:T(8,128)(2,1)}, bf16[1024,1024]{1,0:T(8,128)(2,1)S(1)}, u32[]{:S(2)}, u32[]{:S(2)}) collective-permute-start(bf16[1024,1024]{1,0:T(8,128)(2,1)} %pad_maximum_fusion.4), channel_id=1, source_target_pairs={{0,16},{16,0},{32,48},{48,32},{64,80},{80,64},{96,112},{112,96},{1... | collective-permute-start | bytes 6291464 | tf_op jit(solution)/shard_map/ppermute | solution.py:123
  159.0 1.2 copy-start.5
  167.5 89.6 %all-to-all-start = ((bf16[256,4,1024]{2,1,0:T(4,128)(2,1)}), bf16[256,4,1024]{2,1,0:T(4,128)(2,1)S(1)}, u32[]{:S(2)}, u32[]{:S(2)}) async-start(bf16[256,4,1024]{2,1,0:T(4,128)(2,1)} %convert_element_type.46), calls=%async_computation.1 | async-start | bytes 4194304 | tf_op jit(solution)/shard_map/all_to_all | solution.py:131
Sparse Core Ops, SparseCore 0:
  70.3 69.7 all-gather.1
  159.1 96.2 reduce-scatter.1

commit v8 on v4

--- a/solution.py
+++ b/solution.py
@@ -81,16 +81,28 @@
         return jnp.concatenate([mass_term, damp_term], axis=1)
 
     modal_rows = projected_rows(jnp.int32(0), mode_count, 0)
-    modal_recv = lax.all_to_all(
-        modal_rows.reshape(leaf_count, mode_count // leaf_count, 2 * basis_width).astype(jnp.bfloat16),
+    kept_width = basis_width + mode_count
+    modal_kept = lax.psum_scatter(modal_rows[:, :kept_width], "leaf", scatter_dimension=0, tiled=True)
+    modal_sent = lax.all_to_all(
+        modal_rows[:, kept_width:]
+        .reshape(leaf_count, mode_count // leaf_count, 2 * basis_width - kept_width)
+        .astype(jnp.bfloat16),
         "leaf",
         0,
         0,
         tiled=True,
     )
-    modal_part = jnp.sum(
-        modal_recv.reshape(leaf_count, mode_count // leaf_count, 2 * basis_width).astype(jnp.float32),
-        axis=0,
+    modal_part = jnp.concatenate(
+        [
+            modal_kept,
+            jnp.sum(
+                modal_sent.reshape(
+                    leaf_count, mode_count // leaf_count, 2 * basis_width - kept_width
+                ).astype(jnp.float32),
+                axis=0,
+            ),
+        ],
+        axis=1,
     )
     device_count = group_count * leaf_count
     core_odd = lax.axis_index("group") % 2 == 1

time: 218 us -> 238 us (1.092); the launches traced: 214 us -> 237 us
  waiting for transfers between devices: 103 us -> 113 us
  matrix products: 34.3 us -> 38.4 us
  starting transfers between devices: 13.2 us -> 16.8 us
  other arithmetic: 10.7 us -> 13.5 us
  local copies, waits for them, and re-layouts: 39.1 us -> 41.5 us
    reduce_scatter x0 -> x1, waiting for transfers between devices: none -> 76.5 us  [body(): lax.psum_scatter(modal_rows[:, :kept_width], 'leaf', scatter_dimension=0,...]
    all_to_all x1, waiting for transfers between devices: 44.9 us -> 0.01 us  [body(): lax.all_to_all(root_rows.reshape(device_count, root_width // device_count...]
    all_to_all x1, waiting for transfers between devices: 21.6 us -> 0.75 us  [body(): lax.all_to_all(modal_rows[:, kept_width:].reshape(leaf_count, mode_count...]
    dot_general x6, matrix products: 8.37 us -> 12.4 us  [left_product(): lax.dot_general(first_operand, second_operand, (((0,), (0,)), ((), ())),...]
    unnamed x19 -> x31, local copies, waits for them, and re-layouts: 6.47 us -> 8.58 us
  transfers between devices with their start and end apart: 4 -> 5, of which waited for: 3 -> 3; matrix products, arithmetic and copies ran while one was open for 30% -> 30% of each run, Pallas kernels for 0% -> 0%
where the time goes in v8:
time: 238 us; the launch traced here: 237 us
  waiting for transfers between devices  113 us (47%)
  local copies, waits for them, and re-layouts  41.5 us (17%)
  matrix products  38.4 us (16%)
  starting transfers between devices  16.8 us (7%)
  between operations  14.3 us (6%)
  other arithmetic  13.5 us (6%)
    reduce_scatter x1, waiting for transfers between devices, body(): lax.psum_scatter(modal_rows[:, :kept_width], 'leaf', scatter_dimension=0,...  76.5 us
    all_gather x1, waiting for transfers between devices, body(): mode_basis = lax.all_gather(basis_rows, 'leaf', axis=0, tiled=True)  35.7 us
    convert_element_type x2, local copies, waits for them, and re-layouts, body(): sides = placed[leaf_order:].astype(jnp.float32)  13.3 us
    dot_general x6, matrix products, left_product(): lax.dot_general(first_operand, second_operand, (((0,), (0,)), ((), ())),...  12.4 us
    all_to_all x1, starting transfers between devices, body(): lax.all_to_all(root_rows.reshape(device_count, root_width // device_count...  11.6 us
    concatenate x3, local copies, waits for them, and re-layouts, body(): jnp.concatenate([leaf_modes[0], mass_coupling[0], damp_coupling[0]], axis=0)  9.03 us
    unnamed x31, local copies, waits for them, and re-layouts  8.58 us
    dot_general x1, matrix products, body(): jnp.dot(half_work, mode_basis, preferred_element_type=jnp.float32)  6.61 us
  transfers between devices with their start and end apart: 5, of which 3 were waited for; matrix products, arithmetic and copies ran while one was open for 30% of the time, Pallas kernels for 0%

profile of v8, /device:TPU:2, one launch (start us, length us, event | category | flops | bytes accessed | tf_op | source)
XLA Modules:
  0.0 237.3 jit_solution(3741331215991331386)
XLA Ops:
  7.2 1.6 pad_maximum_fusion.8
  8.9 1.7 copy.26
  10.6 3.0 %copy.29 = bf16[512,12,128]{2,1,0:T(8,128)(2,1)} copy(bf16[512,12,128]{0,2,1:T(8,128)(2,1)S(1)} %bitcast.41) | data formatting | bytes 3145728 | tf_op jit(solution)/shard_map/concatenate | solution.py:47
  13.7 0.7 copy.25
  14.4 3.0 %copy.28 = bf16[512,12,128]{2,1,0:T(8,128)(2,1)} copy(bf16[512,12,128]{0,2,1:T(8,128)(2,1)S(1)} %bitcast.42) | data formatting | bytes 3145728 | tf_op jit(solution)/shard_map/concatenate | solution.py:47
  17.4 0.7 copy.24
  18.1 3.0 %copy.27 = bf16[512,12,128]{2,1,0:T(8,128)(2,1)} copy(bf16[512,12,128]{0,2,1:T(8,128)(2,1)S(1)} %bitcast.43) | data formatting | bytes 3145728 | tf_op jit(solution)/shard_map/concatenate | solution.py:47
  21.1 4.6 %fusion = bf16[12,1536,128]{2,0,1:T(8,128)(2,1)S(1)} fusion(bf16[512,12,128]{2,1,0:T(8,128)(2,1)} %copy.29, bf16[512,12,128]{2,1,0:T(8,128)(2,1)} %copy.28, bf16[512,12,128]{2,1,0:T(8,128)(2,1)} %copy.27, s32[12]{0:T(128)S(1)} %bitcast.50), kind=kOutput, calls=%fused_computation.1 | convolution fusion | flops 70779024 | bytes 9437232 | tf_op jit(solution)/shard_map/lbk,bj->ljk/dot_general | solution.py:9
  25.7 1.2 copy.38
  27.0 2.2 copy-done.1
  29.2 0.1 slice.90
  29.3 0.7 copy.31
  30.0 5.1 %slice_convert_fusion = f32[1024,12,128]{2,0,1:T(8,128)} fusion(bf16[1536,12,128]{2,0,1:T(8,128)(2,1)} %bitcast.39), kind=kLoop, calls=%fused_computation.14 | loop fusion | flops 1572864 | bytes 9437184 | tf_op jit(solution)/shard_map/convert_element_type | solution.py:53
  35.2 6.6 %copy.32 = f32[1024,12,128]{0,2,1:T(8,128)} copy(f32[1024,12,128]{2,0,1:T(8,128)} %slice_convert_fusion) | data formatting | bytes 12582912 | tf_op jit(solution)/shard_map/convert_element_type | solution.py:53
  41.8 6.7 %copy.33 = f32[1024,1536]{1,0:T(8,128)} copy(f32[1024,1536]{0,1:T(8,128)} %bitcast.37) | data formatting | bytes 12582912 | tf_op jit(solution)/shard_map/convert_element_type | solution.py:53
  48.5 4.4 %fusion.14 = f32[1024,1536]{1,0:T(8,128)} fusion(bf16[512,1536]{0,1:T(8,128)(2,1)S(1)} %bitcast.44, bf16[512,512]{1,0:T(8,128)(2,1)S(1)} %bitcast.48, bf16[512,512]{1,0:T(8,128)(2,1)S(1)} %bitcast.49), kind=kOutput, calls=%fused_computation.29 | convolution fusion | flops 1612709888 | bytes 8912896 | tf_op jit(solution)/shard_map/dot_general | solution.py:54
  52.9 35.7 %all-gather.2.cloned.1.call-done = bf16[1536,1280]{1,0:T(8,128)(2,1)} async-done(((bf16[96,1280]{1,0:T(8,128)(2,1)}), bf16[1536,1280]{1,0:T(8,128)(2,1)}) %all-gather.2.cloned.1.call-update) | async-done | bytes 3932176 | tf_op jit(solution)/shard_map/all_gather | solution.py:62
  88.6 4.5 %convolution_convert_fusion.1 = bf16[512,1280]{1,0:T(8,128)(2,1)S(1)} fusion(bf16[512,1536]{0,1:T(8,128)(2,1)S(1)} %bitcast.45, bf16[1536,1280]{1,0:T(8,128)(2,1)} %all-gather.2.cloned.1.call-done), kind=kOutput, calls=%fused_computation.16 | convolution fusion | flops 2013921280 | bytes 6815744 | tf_op jit(solution)/shard_map/dot_general | solution.py:63
  93.1 0.1 slice.101
  93.2 1.1 copy-done.5
  94.4 6.6 %convolution_convert_fusion = bf16[1024,1280]{1,0:T(8,128)(2,1)S(1)} fusion(bf16[1536,1280]{1,0:T(8,128)(2,1)} %all-gather.2.cloned.1.call-done, f32[1024,1536]{1,0:T(8,128)S(1)} %copy-done, f32[1024,1536]{1,0:T(8,128)S(1)} %copy-done.5), kind=kOutput, calls=%fused_computation.12 | convolution fusion | flops 4032561152 | bytes 19136512 | tf_op jit(solution)/shard_map/dot_general | solution.py:64
  101.0 1.3 broadcast_select_fusion
  102.2 1.6 pad_maximum_fusion
  103.8 0.5 fusion.10
  104.4 0.5 convolution_add_fusion
  104.9 1.1 copy-done.3
  106.0 0.9 slice.129
  106.9 4.9 %all-to-all-start = ((bf16[16,16,1024]{2,1,0:T(8,128)(2,1)}), bf16[16,16,1024]{2,1,0:T(8,128)(2,1)S(1)}, u32[]{:S(2)}, u32[]{:S(2)}) async-start(bf16[16,16,1024]{2,1,0:T(8,128)(2,1)} %bitcast.15), calls=%async_computation.1 | async-start | bytes 1048576 | tf_op jit(solution)/shard_map/all_to_all | solution.py:86
  111.8 3.0 %fusion.12 = f32[256,1280]{1,0:T(8,128)} fusion(bf16[1024,1280]{1,0:T(8,128)(2,1)} %copy-done.2, bf16[512,1280]{1,0:T(8,128)(2,1)S(1)} %convolution_convert_fusion.1), kind=kOutput, calls=%fused_computation.26 | convolution fusion | flops 335544320 | bytes 2883584 | tf_op jit(solution)/shard_map/dot_general | solution.py:19
  114.8 1.8 fusion.32
  116.6 0.0 copy-done.10
  116.6 2.4 %fusion.9 = f32[1024,1024]{1,0:T(8,128)S(1)} fusion(bf16[512,1024]{1,0:T(8,128)(2,1)S(1)} %get-tuple-element.9, bf16[512,1024]{1,0:T(8,128)(2,1)S(1)} %copy-done.10, bf16[512,1024]{1,0:T(8,128)(2,1)S(1)} %slice.101, bf16[512,1024]{1,0:T(8,128)(2,1)S(1)} %get-tuple-element.8), kind=kOutput, calls=%fused_computation.23 | convolution fusion | flops 2155872256 | bytes 8388608 | tf_op jit(solution)/shard_map/dot_general | solution.py:19
  119.0 3.9 %add_convert_fusion.2 = bf16[1024,1024]{1,0:T(8,128)(2,1)} fusion(f32[1024,1024]{1,0:T(8,128)S(1)} %fusion.9, bf16[512,1024]{1,0:T(8,128)(2,1)S(1)} %get-tuple-element.9, bf16[512,1024]{1,0:T(8,128)(2,1)S(1)} %copy-done.10, bf16[512,1024]{1,0:T(8,128)(2,1)S(1)} %slice.101, bf16[512,1024]{1,0:T(8,128)(2,1)S(1)} %get-tuple-element.8), kind=kOutput, calls=%fused_computation.11 | convolution fusion | flops 2157969408 | bytes 10485760 | tf_op jit(solution)/shard_map/dot_general | solution.py:19
  123.0 4.1 %convert_element_type.55 = bf16[256,4,1024]{2,1,0:T(4,128)(2,1)} reshape(bf16[1024,1024]{1,0:T(8,128)(2,1)} %add_convert_fusion.2) | data formatting | bytes 4194304 | tf_op jit(solution)/shard_map/convert_element_type | solution.py:123
  127.1 0.8 all-to-all-done
  127.8 0.8 copy-done.6
  128.7 11.6 %all-to-all-start.1 = ((bf16[256,4,1024]{2,1,0:T(4,128)(2,1)}), bf16[256,4,1024]{2,1,0:T(4,128)(2,1)S(1)}, u32[]{:S(2)}, u32[]{:S(2)}) async-start(bf16[256,4,1024]{2,1,0:T(4,128)(2,1)} %convert_element_type.55), calls=%async_computation.2 | async-start | bytes 4194304 | tf_op jit(solution)/shard_map/all_to_all | solution.py:122
  140.3 0.3 reduce-scatter.2.cloned.1.call-start
  140.5 2.0 convolution_add_fusion.1
  142.6 1.3 pad_maximum_fusion.3
  143.9 5.7 %fusion.7 = f32[1024,256]{1,0:T(8,128)S(1)} fusion(f32[1024,1536]{1,0:T(8,128)} %fusion.14, f32[1024,1536]{1,0:T(8,128)} %copy.33, bf16[1536,1280]{1,0:T(8,128)(2,1)} %all-gather.2.cloned.1.call-done), kind=kOutput, calls=%fused_computation.13 | convolution fusion | flops 808452096 | bytes 14417920 | tf_op jit(solution)/shard_map/dot_general | solution.py:65
  149.7 1.0 slice_bitcast_fusion
  150.7 0.2 copy-done.7
  150.9 0.1 convert_reduce_fusion.1
  151.0 76.5 %reduce-scatter.2.cloned.1.call-done = f32[16,1536]{1,0:T(8,128)} async-done(((f32[256,1536]{1,0:T(8,128)}), f32[16,1536]{1,0:T(8,128)}) %reduce-scatter.2.cloned.1.call-update) | async-done | bytes 98320 | tf_op jit(solution)/shard_map/reduce_scatter | solution.py:85
  227.4 1.6 fusion.23
  229.0 0.8 convert_reduce_fusion
  229.9 0.6 slice_bitcast_fusion.3
  (28 shorter events, 0.1 us)
Async XLA Ops:
  7.2 81.4 %all-gather.2.cloned.1.call-start = ((), (), s32[]{:S(2)}) async-start(), calls=%async_computation.3 | async-start | bytes 4177920 | tf_op jit(solution)/shard_map/all_gather | solution.py:62
  10.6 3.0 %copy-start.8 = (bf16[1,512,1536]{2,1,0:T(8,128)(2,1)S(1)}, bf16[1,512,1536]{2,1,0:T(8,128)(2,1)}, u32[]{:S(2)}) copy-start(bf16[1,512,1536]{2,1,0:T(8,128)(2,1)} %param.10) | copy-start | bytes 4718596
  14.4 3.0 %copy-start.9 = (bf16[1,512,1536]{2,1,0:T(8,128)(2,1)S(1)}, bf16[1,512,1536]{2,1,0:T(8,128)(2,1)}, u32[]{:S(2)}) copy-start(bf16[1,512,1536]{2,1,0:T(8,128)(2,1)} %param.12) | copy-start | bytes 4718596
  18.1 3.0 %copy-start.13 = (s32[1,12]{1,0:T(1,128)S(1)}, s32[1,12]{1,0:T(1,128)}, u32[]{:S(2)}) copy-start(s32[1,12]{1,0:T(1,128)} %param.13) | copy-start | bytes 148
  27.0 2.2 copy-start.1
  41.8 6.7 %copy-start.11 = (bf16[1,512,512]{2,1,0:T(8,128)(2,1)S(1)}, bf16[1,512,512]{2,1,0:T(8,128)(2,1)}, u32[]{:S(2)}) copy-start(bf16[1,512,512]{2,1,0:T(8,128)(2,1)} %param.9) | copy-start | bytes 1572868
  41.8 6.7 %copy-start.12 = (bf16[1,512,512]{2,1,0:T(8,128)(2,1)S(1)}, bf16[1,512,512]{2,1,0:T(8,128)(2,1)}, u32[]{:S(2)}) copy-start(bf16[1,512,512]{2,1,0:T(8,128)(2,1)} %param.8) | copy-start | bytes 1572868
  88.6 4.7 %copy-start = (f32[1024,1536]{1,0:T(8,128)S(1)}, f32[1024,1536]{1,0:T(8,128)}, u32[]{:S(2)}) copy-start(f32[1024,1536]{1,0:T(8,128)} %copy.33) | copy-start | bytes 18874372
  88.6 5.8 %copy-start.5 = (f32[1024,1536]{1,0:T(8,128)S(1)}, f32[1024,1536]{1,0:T(8,128)}, u32[]{:S(2)}) copy-start(f32[1024,1536]{1,0:T(8,128)} %fusion.14) | copy-start | bytes 18874372
  101.0 3.4 %copy-start.2 = (bf16[1024,1280]{1,0:T(8,128)(2,1)}, bf16[1024,1280]{1,0:T(8,128)(2,1)S(1)}, u32[]{:S(2)}) copy-start(bf16[1024,1280]{1,0:T(8,128)(2,1)S(1)} %convolution_convert_fusion) | copy-start | bytes 7864324
  103.8 10.9 %collective-permute-start = (bf16[1024,1024]{1,0:T(8,128)(2,1)}, bf16[1024,1024]{1,0:T(8,128)(2,1)}, u32[]{:S(2)}, u32[]{:S(2)}) collective-permute-start(bf16[1024,1024]{1,0:T(8,128)(2,1)} %pad_maximum_fusion), channel_id=1, source_target_pairs={{0,16},{16,0},{32,48},{48,32},{64,80},{80,64},{96,112},{112,96},{1... | collective-permute-start | bytes 6291464 | tf_op jit(solution)/shard_map/ppermute | solution.py:114
  104.9 1.1 copy-start.3
  106.9 21.0 %all-to-all-start = ((bf16[16,16,1024]{2,1,0:T(8,128)(2,1)}), bf16[16,16,1024]{2,1,0:T(8,128)(2,1)S(1)}, u32[]{:S(2)}, u32[]{:S(2)}) async-start(bf16[16,16,1024]{2,1,0:T(8,128)(2,1)} %bitcast.15), calls=%async_computation.1 | async-start | bytes 1048576 | tf_op jit(solution)/shard_map/all_to_all | solution.py:86
  114.7 1.9 copy-start.10
  127.8 0.8 copy-start.6
  128.7 100.4 %all-to-all-start.1 = ((bf16[256,4,1024]{2,1,0:T(4,128)(2,1)}), bf16[256,4,1024]{2,1,0:T(4,128)(2,1)S(1)}, u32[]{:S(2)}, u32[]{:S(2)}) async-start(bf16[256,4,1024]{2,1,0:T(4,128)(2,1)} %convert_element_type.55), calls=%async_computation.2 | async-start | bytes 4194304 | tf_op jit(solution)/shard_map/all_to_all | solution.py:122
  140.3 87.2 %reduce-scatter.2.cloned.1.call-start = ((), (), s32[]{:S(2)}) async-start(), calls=%async_computation.4 | async-start | bytes 1671168 | tf_op jit(solution)/shard_map/reduce_scatter | solution.py:85
  140.5 2.1 copy-start.4
  149.7 1.2 copy-start.7
Sparse Core Ops, SparseCore 0:
  10.3 78.1 all-gather.1
  144.1 83.3 reduce-scatter.1

commit v9 on v6

--- a/solution.py
+++ b/solution.py
@@ -80,14 +80,15 @@
         )
         return jnp.concatenate([mass_term, damp_term], axis=1)
 
-    modal_part = lax.psum_scatter(
-        projected_rows(jnp.int32(0), mode_count, 0), "leaf", scatter_dimension=0, tiled=True
+    modal_rows, left_ready, mass_ready, damp_ready = lax.optimization_barrier(
+        (projected_rows(jnp.int32(0), mode_count, 0), left_part, right_mass, right_damp)
     )
+    modal_part = lax.psum_scatter(modal_rows, "leaf", scatter_dimension=0, tiled=True)
     device_count = group_count * leaf_count
     core_odd = lax.axis_index("group") % 2 == 1
-    left_root = left_part[:, mode_count:]
-    mass_root = right_mass[:, mode_count:]
-    damp_root = right_damp[:, mode_count:]
+    left_root = left_ready[:, mode_count:]
+    mass_root = mass_ready[:, mode_count:]
+    damp_root = damp_ready[:, mode_count:]
     own_right = jnp.where(core_odd, damp_root, mass_root)
     other_right = jnp.where(core_odd, mass_root, damp_root)
     partner = lax.ppermute(

time: 215 us -> 218 us (1.014)
    ppermute x1, waiting for transfers between devices: 0.4 us -> 4.32 us  [body(): lax.ppermute(jnp.concatenate([left_root, other_right], axis=0), 'group',...]
    reduce_scatter x1, waiting for transfers between devices: 71.7 us -> 68.6 us  [body(): lax.psum_scatter(modal_rows, 'leaf', scatter_dimension=0, tiled=True)]
    unnamed x21 -> x27, local copies, waits for them, and re-layouts: 7.11 us -> 7.88 us
  transfers between devices with their start and end apart: 4 -> 4, of which waited for: 3 -> 3; matrix products, arithmetic and copies ran while one was open for 29% -> 26% of each run, Pallas kernels for 0% -> 0%
where the time goes in v9:
time: 218 us; the launch traced here: 217 us
  waiting for transfers between devices  109 us (50%)
  local copies, waits for them, and re-layouts  39.2 us (18%)
  matrix products  33.1 us (15%)
  between operations  14.3 us (7%)
  other arithmetic  12.2 us (6%)
  starting transfers between devices  9.77 us (4%)
    reduce_scatter x1, waiting for transfers between devices, body(): lax.psum_scatter(modal_rows, 'leaf', scatter_dimension=0, tiled=True)  68.6 us
    all_gather x1, waiting for transfers between devices, body(): mode_basis = lax.all_gather(basis_rows, 'leaf', axis=0, tiled=True)  35.6 us
    convert_element_type x2, local copies, waits for them, and re-layouts, body(): sides = placed[leaf_order:].astype(jnp.float32)  13.3 us
    all_to_all x1, starting transfers between devices, body(): lax.all_to_all(root_rows.reshape(device_count, root_width // device_count...  9.69 us
    concatenate x3, local copies, waits for them, and re-layouts, body(): jnp.concatenate([leaf_modes[0], mass_coupling[0], damp_coupling[0]], axis=0)  9.03 us
    unnamed x27, local copies, waits for them, and re-layouts  7.88 us
    dot_general x6, matrix products, left_product(): lax.dot_general(first_operand, second_operand, (((0,), (0,)), ((), ())),...  7.12 us
    dot_general x1, matrix products, body(): jnp.dot(half_work, mode_basis, preferred_element_type=jnp.float32)  6.61 us
  transfers between devices with their start and end apart: 4, of which 3 were waited for; matrix products, arithmetic and copies ran while one was open for 26% of the time, Pallas kernels for 0%

profile of v9, /device:TPU:2, one launch (start us, length us, event | category | flops | bytes accessed | tf_op | source)
XLA Modules:
  0.0 217.1 jit_solution(15674081019871585092)
XLA Ops:
  7.2 0.0 all-gather.2.cloned.1.call-start
  7.2 1.6 pad_maximum_fusion.8
  8.9 0.0 all-gather.2.cloned.1.call-update
  8.9 0.0 reduce-scatter.2.cloned.1.call-start
  8.9 1.7 copy.26
  10.7 0.0 copy-start.6
  10.7 3.0 %copy.29 = bf16[512,12,128]{2,1,0:T(8,128)(2,1)} copy(bf16[512,12,128]{0,2,1:T(8,128)(2,1)S(1)} %bitcast.40) | data formatting | bytes 3145728 | tf_op jit(solution)/shard_map/concatenate | solution.py:47
  13.7 0.7 copy.25
  14.4 3.0 %copy.28 = bf16[512,12,128]{2,1,0:T(8,128)(2,1)} copy(bf16[512,12,128]{0,2,1:T(8,128)(2,1)S(1)} %bitcast.41) | data formatting | bytes 3145728 | tf_op jit(solution)/shard_map/concatenate | solution.py:47
  17.4 0.7 copy.24
  18.1 3.0 %copy.27 = bf16[512,12,128]{2,1,0:T(8,128)(2,1)} copy(bf16[512,12,128]{0,2,1:T(8,128)(2,1)S(1)} %bitcast.42) | data formatting | bytes 3145728 | tf_op jit(solution)/shard_map/concatenate | solution.py:47
  21.1 4.6 %fusion = bf16[12,1536,128]{2,0,1:T(8,128)(2,1)S(1)} fusion(bf16[512,12,128]{2,1,0:T(8,128)(2,1)} %copy.29, bf16[512,12,128]{2,1,0:T(8,128)(2,1)} %copy.28, bf16[512,12,128]{2,1,0:T(8,128)(2,1)} %copy.27, s32[12]{0:T(128)S(1)} %bitcast.49), kind=kOutput, calls=%fused_computation.1 | convolution fusion | flops 70779024 | bytes 9437232 | tf_op jit(solution)/shard_map/lbk,bj->ljk/dot_general | solution.py:9
  25.8 1.2 copy.38
  27.0 2.2 %copy-done.1 = bf16[12,1536,128]{2,1,0:T(8,128)(2,1)} copy-done((bf16[12,1536,128]{2,1,0:T(8,128)(2,1)}, bf16[12,1536,128]{2,1,0:T(8,128)(2,1)S(1)}, u32[]{:S(2)}) %copy-start.1) | copy-done | bytes 4718616
  29.3 0.1 slice.79
  29.4 0.7 copy.31
  30.1 5.1 %slice_convert_fusion = f32[1024,12,128]{2,0,1:T(8,128)} fusion(bf16[1536,12,128]{2,0,1:T(8,128)(2,1)} %bitcast.38), kind=kLoop, calls=%fused_computation.14 | loop fusion | flops 1572864 | bytes 9437184 | tf_op jit(solution)/shard_map/convert_element_type | solution.py:53
  35.2 6.6 %copy.32 = f32[1024,12,128]{0,2,1:T(8,128)} copy(f32[1024,12,128]{2,0,1:T(8,128)} %slice_convert_fusion) | data formatting | bytes 12582912 | tf_op jit(solution)/shard_map/convert_element_type | solution.py:53
  41.8 6.7 %copy.33 = f32[1024,1536]{1,0:T(8,128)} copy(f32[1024,1536]{0,1:T(8,128)} %bitcast.36) | data formatting | bytes 12582912 | tf_op jit(solution)/shard_map/convert_element_type | solution.py:53
  48.5 4.4 %fusion.10 = f32[1024,1536]{1,0:T(8,128)} fusion(bf16[512,1536]{0,1:T(8,128)(2,1)S(1)} %bitcast.43, bf16[512,512]{1,0:T(8,128)(2,1)S(1)} %bitcast.47, bf16[512,512]{1,0:T(8,128)(2,1)S(1)} %bitcast.48), kind=kOutput, calls=%fused_computation.24 | convolution fusion | flops 1612709888 | bytes 8912896 | tf_op jit(solution)/shard_map/dot_general | solution.py:54
  53.0 35.6 %all-gather.2.cloned.1.call-done = bf16[1536,1280]{1,0:T(8,128)(2,1)} async-done(((bf16[96,1280]{1,0:T(8,128)(2,1)}), bf16[1536,1280]{1,0:T(8,128)(2,1)}) %all-gather.2.cloned.1.call-update) | async-done | bytes 3932176 | tf_op jit(solution)/shard_map/all_gather | solution.py:62
  88.6 4.5 %convolution_convert_fusion.1 = bf16[512,1280]{1,0:T(8,128)(2,1)S(1)} fusion(bf16[512,1536]{0,1:T(8,128)(2,1)S(1)} %bitcast.44, bf16[1536,1280]{1,0:T(8,128)(2,1)} %all-gather.2.cloned.1.call-done), kind=kOutput, calls=%fused_computation.16 | convolution fusion | flops 2013921280 | bytes 6815744 | tf_op jit(solution)/shard_map/dot_general | solution.py:63
  93.1 1.3 copy-done.2
  94.4 6.6 %convolution_convert_fusion = bf16[1024,1280]{1,0:T(8,128)(2,1)S(1)} fusion(bf16[1536,1280]{1,0:T(8,128)(2,1)} %all-gather.2.cloned.1.call-done, f32[1024,1536]{1,0:T(8,128)S(1)} %copy-done, f32[1024,1536]{1,0:T(8,128)S(1)} %copy-done.2), kind=kOutput, calls=%fused_computation.12 | convolution fusion | flops 4032561152 | bytes 19136512 | tf_op jit(solution)/shard_map/dot_general | solution.py:64
  101.0 0.5 fusion.17
  101.5 0.5 fusion.19
  102.0 1.2 fusion.31
  103.3 0.5 convolution_add_fusion
  103.8 0.5 convolution_add_fusion.1
  104.4 1.8 pad_maximum_fusion
  106.2 0.1 slice.72
  106.3 1.2 copy-done.3
  107.5 1.3 broadcast_select_fusion
  108.8 0.1 copy-done.4
  108.8 1.5 pad_maximum_fusion.1
  110.3 0.0 reduce-scatter.2.cloned.1.call-update
  110.4 4.3 %collective-permute-done = bf16[1024,1024]{1,0:T(8,128)(2,1)S(1)} collective-permute-done((bf16[1024,1024]{1,0:T(8,128)(2,1)}, bf16[1024,1024]{1,0:T(8,128)(2,1)S(1)}, u32[]{:S(2)}, u32[]{:S(2)}) %collective-permute-start) | collective-permute-done | bytes 2097184 | tf_op jit(solution)/shard_map/ppermute | solution.py:94
  114.7 0.2 fusion.32
  114.9 2.4 %fusion.9 = f32[1024,1024]{1,0:T(8,128)S(1)} fusion(bf16[512,1024]{1,0:T(8,128)(2,1)S(1)} %get-tuple-element.19, bf16[512,1024]{1,0:T(8,128)(2,1)S(1)} %copy-done.8, bf16[512,1024]{1,0:T(8,128)(2,1)S(1)} %copy-done.5, bf16[512,1024]{1,0:T(8,128)(2,1)S(1)} %get-tuple-element.18), kind=kOutput, calls=%fused_computation.23 | convolution fusion | flops 2155872256 | bytes 8388608 | tf_op jit(solution)/shard_map/dot_general | solution.py:19
  117.3 2.6 %add_convert_fusion.2 = bf16[1024,1024]{1,0:T(8,128)(2,1)S(1)} fusion(f32[1024,1024]{1,0:T(8,128)S(1)} %fusion.9, bf16[512,1024]{1,0:T(8,128)(2,1)S(1)} %get-tuple-element.19, bf16[512,1024]{1,0:T(8,128)(2,1)S(1)} %copy-done.8, bf16[512,1024]{1,0:T(8,128)(2,1)S(1)} %copy-done.5, bf16[512,1024]{1,0:T(8,128)(2,1)S(1)} %get-tuple-element.18), kind=kOutput, calls=%fused_computation.11 | convolution fusion | flops 2157969408 | bytes 10485760 | tf_op jit(solution)/shard_map/dot_general | solution.py:19
  119.9 2.2 %convert_element_type.46 = bf16[256,4,1024]{2,1,0:T(4,128)(2,1)} reshape(bf16[1024,1024]{1,0:T(8,128)(2,1)S(1)} %add_convert_fusion.2) | data formatting | bytes 4194304 | tf_op jit(solution)/shard_map/convert_element_type | solution.py:103
  122.1 9.7 %all-to-all-start = ((bf16[256,4,1024]{2,1,0:T(4,128)(2,1)}), bf16[256,4,1024]{2,1,0:T(4,128)(2,1)S(1)}, u32[]{:S(2)}, u32[]{:S(2)}) async-start(bf16[256,4,1024]{2,1,0:T(4,128)(2,1)} %convert_element_type.46), calls=%async_computation.1 | async-start | bytes 4194304 | tf_op jit(solution)/shard_map/all_to_all | solution.py:102
  131.8 5.8 %fusion.7 = f32[1024,256]{1,0:T(8,128)S(1)} fusion(f32[1024,1536]{1,0:T(8,128)} %fusion.10, f32[1024,1536]{1,0:T(8,128)} %copy.33, bf16[1536,1280]{1,0:T(8,128)(2,1)} %all-gather.2.cloned.1.call-done), kind=kOutput, calls=%fused_computation.13 | convolution fusion | flops 808452096 | bytes 14417920 | tf_op jit(solution)/shard_map/dot_general | solution.py:65
  137.6 1.0 slice_bitcast_fusion
  138.6 68.6 %reduce-scatter.2.cloned.1.call-done = f32[16,2560]{1,0:T(8,128)} async-done(((f32[256,2560]{1,0:T(8,128)}), f32[16,2560]{1,0:T(8,128)}) %reduce-scatter.2.cloned.1.call-update) | async-done | bytes 163856 | tf_op jit(solution)/shard_map/reduce_scatter | solution.py:86
  207.2 1.6 slice_bitcast_fusion.2
  208.8 0.8 convert_reduce_fusion
  209.7 0.6 slice_bitcast_fusion.4
  (21 shorter events, 0.0 us)
Async XLA Ops:
  7.2 81.4 %all-gather.2.cloned.1.call-start = ((), (), s32[]{:S(2)}) async-start(), calls=%async_computation.2 | async-start | bytes 4177920 | tf_op jit(solution)/shard_map/all_gather | solution.py:62
  8.9 198.4 %reduce-scatter.2.cloned.1.call-start = ((), (), s32[]{:S(2)}) async-start(), calls=%async_computation.3 | async-start | bytes 2785280 | tf_op jit(solution)/shard_map/reduce_scatter | solution.py:86
  10.7 3.0 %copy-start.6 = (bf16[1,512,1536]{2,1,0:T(8,128)(2,1)S(1)}, bf16[1,512,1536]{2,1,0:T(8,128)(2,1)}, u32[]{:S(2)}) copy-start(bf16[1,512,1536]{2,1,0:T(8,128)(2,1)} %param.10) | copy-start | bytes 4718596
  14.4 3.0 %copy-start.7 = (bf16[1,512,1536]{2,1,0:T(8,128)(2,1)S(1)}, bf16[1,512,1536]{2,1,0:T(8,128)(2,1)}, u32[]{:S(2)}) copy-start(bf16[1,512,1536]{2,1,0:T(8,128)(2,1)} %param.12) | copy-start | bytes 4718596
  18.1 3.0 %copy-start.11 = (s32[1,12]{1,0:T(1,128)S(1)}, s32[1,12]{1,0:T(1,128)}, u32[]{:S(2)}) copy-start(s32[1,12]{1,0:T(1,128)} %param.13) | copy-start | bytes 148
  27.0 2.2 %copy-start.1 = (bf16[12,1536,128]{2,1,0:T(8,128)(2,1)}, bf16[12,1536,128]{2,1,0:T(8,128)(2,1)S(1)}, u32[]{:S(2)}) copy-start(bf16[12,1536,128]{2,1,0:T(8,128)(2,1)S(1)} %copy.38) | copy-start | bytes 14155780
  41.8 6.7 %copy-start.9 = (bf16[1,512,512]{2,1,0:T(8,128)(2,1)S(1)}, bf16[1,512,512]{2,1,0:T(8,128)(2,1)}, u32[]{:S(2)}) copy-start(bf16[1,512,512]{2,1,0:T(8,128)(2,1)} %param.9) | copy-start | bytes 1572868
  41.8 6.7 %copy-start.10 = (bf16[1,512,512]{2,1,0:T(8,128)(2,1)S(1)}, bf16[1,512,512]{2,1,0:T(8,128)(2,1)}, u32[]{:S(2)}) copy-start(bf16[1,512,512]{2,1,0:T(8,128)(2,1)} %param.8) | copy-start | bytes 1572868
  88.6 4.5 %copy-start = (f32[1024,1536]{1,0:T(8,128)S(1)}, f32[1024,1536]{1,0:T(8,128)}, u32[]{:S(2)}) copy-start(f32[1024,1536]{1,0:T(8,128)} %copy.33) | copy-start | bytes 18874372
  88.6 5.8 %copy-start.2 = (f32[1024,1536]{1,0:T(8,128)S(1)}, f32[1024,1536]{1,0:T(8,128)}, u32[]{:S(2)}) copy-start(f32[1024,1536]{1,0:T(8,128)} %fusion.10) | copy-start | bytes 18874372
  106.2 1.3 copy-start.3
  107.5 1.3 copy-start.4
  110.3 4.4 %collective-permute-start = (bf16[1024,1024]{1,0:T(8,128)(2,1)}, bf16[1024,1024]{1,0:T(8,128)(2,1)S(1)}, u32[]{:S(2)}, u32[]{:S(2)}) collective-permute-start(bf16[1024,1024]{1,0:T(8,128)(2,1)} %pad_maximum_fusion.1), channel_id=1, source_target_pairs={{0,16},{16,0},{32,48},{48,32},{64,80},{80,64},{96,112},{112,96},{1... | collective-permute-start | bytes 6291464 | tf_op jit(solution)/shard_map/ppermute | solution.py:94
  110.3 4.5 %copy-start.5 = (bf16[512,1024]{1,0:T(8,128)(2,1)S(1)}, bf16[512,1024]{1,0:T(8,128)(2,1)}, u32[]{:S(2)}) copy-start(bf16[512,1024]{1,0:T(8,128)(2,1)} %copy-done.4) | copy-start | bytes 3145732
  110.4 4.5 %copy-start.8 = (bf16[512,1024]{1,0:T(8,128)(2,1)S(1)}, bf16[512,1024]{1,0:T(8,128)(2,1)}, u32[]{:S(2)}) copy-start(bf16[512,1024]{1,0:T(8,128)(2,1)} %get-tuple-element.14) | copy-start | bytes 3145732
  122.1 86.7 %all-to-all-start = ((bf16[256,4,1024]{2,1,0:T(4,128)(2,1)}), bf16[256,4,1024]{2,1,0:T(4,128)(2,1)S(1)}, u32[]{:S(2)}, u32[]{:S(2)}) async-start(bf16[256,4,1024]{2,1,0:T(4,128)(2,1)} %convert_element_type.46), calls=%async_computation.1 | async-start | bytes 4194304 | tf_op jit(solution)/shard_map/all_to_all | solution.py:102
Sparse Core Ops, SparseCore 0:
  10.3 78.1 all-gather.1
  110.5 96.7 reduce-scatter.1
